TPU v7x, 512 devices: a whole 4x4x16 slice. The times are simulated.
512 devices in a mesh: wide: 128 (over y, z, core), narrow: 4 (over x).
Axes of the slice: x: 4, y: 4, z: 16, core: 2. Of those that a mesh axis runs over, the one named last changes fastest.
Arguments:
- rhs: float32 [512, 65536], P(None, ('wide', 'narrow')), may hold values from -20 to 20
- levels: int32 [65536], P(('wide', 'narrow')), may hold values from 0 to 3
- face_source: int32 [6, 65536], P(None, ('wide', 'narrow')), may hold values from -1 to 1343, as said below
- subface: int32 [6, 65536], P(None, ('wide', 'narrow')), may hold values from 0 to 4
- orientation: int32 [6, 65536], P(None, ('wide', 'narrow')), may hold values from 0 to 7
- send_list: int32 [512, 576], P(('wide', 'narrow')), may hold values from 0 to 767
- parent: int32 [128, 512], P('wide', 'narrow'), may hold values from 0 to 127, never falling along the last dimension, each value on 1 to 8 neighbouring positions
- coarse_inverse: float32 [128, 128, 128], P('wide'), may hold values from -1.5 to 1.5, as said below
Outputs:
- corrected: float32 [512, 65536], P(None, ('wide', 'narrow'))
- residual: float32 [512, 65536], P(None, ('wide', 'narrow'))
Inputs may be any that keep to these rules, and one draw needn't show every extreme that they name: `face_source`: exactly 288 faces of each device name a source device and slot, no slot twice; sources lie in the device's own block or in the blocks just before and after it along wide, never outside the mesh; every device names all 48 slots of some device of its own block; -1 marks a boundary face. `coarse_inverse`: diagonal entries lie in 0.5 to 1.5.
All inputs are finite; a program needn't handle non-finite values.
Results may differ from a plain program's by a relative error of at most 0.00023.
Values sent between devices are 32-bit elements; how exact they have to be, the bound alone decides.
No kernel may reach another device: no remote copies, remote signals or barrier semaphores. Data moves between devices by JAX's collectives and lax.ppermute only.
A program may use at most 64 MiB of HBM per device.

v0:
```python
import jax
import jax.numpy as jnp
import numpy as np
from jax import lax
from jax.sharding import PartitionSpec as P

NODES = 8
POWER = 3
CHEB = 4


PENALTY = 32.0
SAFETY = 1.2
RANGE_RATIO = 8.0
HIGHEST = lax.Precision.HIGHEST


def legendre_rows(points, count):
    rows_list = [points * 0.0 + 1.0, points.copy()]
    for order in range(2, count):
        rows_list.append(
            ((2 * order - 1) * points * rows_list[order - 1] - (order - 1) * rows_list[order - 2])
            / order
        )
    return rows_list


def gll_tables(count):
    degree_top = count - 1
    node_pos = np.cos(np.pi * np.arange(count) / degree_top)
    for newton_step in range(60):
        values_table = legendre_rows(node_pos, count)
        node_pos = node_pos - (
            node_pos * values_table[degree_top] - values_table[degree_top - 1]
        ) / (count * values_table[degree_top])
    node_pos = node_pos[::-1].copy()
    node_pos[0] = -1.0
    node_pos[-1] = 1.0
    values_table = legendre_rows(node_pos, count)
    weights = 2.0 / (degree_top * count * values_table[degree_top] ** 2)
    barycentric = np.array(
        [
            1.0 / np.prod([node_pos[j] - node_pos[k] for k in range(count) if k != j])
            for j in range(count)
        ]
    )
    derivative = np.zeros((count, count))
    for i in range(count):
        for j in range(count):
            if i != j:
                derivative[i, j] = barycentric[j] / barycentric[i] / (node_pos[i] - node_pos[j])
        derivative[i, i] = -np.sum(derivative[i])
    stiffness = derivative.T @ (weights[:, None] * derivative)

    def interpolate(targets):
        matrix = np.ones((count, count))
        for j in range(count):
            for k in range(count):
                if k != j:
                    matrix[:, j] *= (targets - node_pos[k]) / (node_pos[j] - node_pos[k])
        return matrix

    half_low = interpolate((node_pos - 1.0) / 2.0)
    half_high = interpolate((node_pos + 1.0) / 2.0)
    return tuple(
        (
            jnp.asarray(table, dtype=jnp.float32)
            for table in (weights, stiffness, half_low, half_high)
        )
    )


def face_traces(cube):
    return jnp.stack([cube[0], cube[-1], cube[:, 0], cube[:, -1], cube[:, :, 0], cube[:, :, -1]])


def add_faces(cube, values):
    count = cube.shape[0]
    first = (jnp.arange(count) == 0).astype(cube.dtype)
    last = (jnp.arange(count) == count - 1).astype(cube.dtype)
    for index in range(6):
        axis, pick = index // 2, (first, last)[index % 2]
        shape = [1] * cube.ndim
        shape[axis] = count
        cube = cube + pick.reshape(shape) * jnp.expand_dims(values[index], axis)
    return cube


def orient_faces(neighbour, orientation, subface, half_low, half_high):
    bit_one = (orientation % 2)[:, None, None, :] == 1
    bit_two = (orientation // 2 % 2)[:, None, None, :] == 1
    bit_four = (orientation // 4)[:, None, None, :] == 1
    turned = jnp.where(bit_one, neighbour[:, ::-1], neighbour)
    turned = jnp.where(bit_two, turned[:, :, ::-1], turned)
    turned = jnp.where(bit_four, jnp.swapaxes(turned, 1, 2), turned)
    hanging = (subface > 0)[:, None, None, :]
    quad_first = ((subface - 1) % 2)[:, None, None, :] == 0
    quad_second = ((subface - 1) // 2)[:, None, None, :] == 0
    low_first = jnp.einsum("ai,fibe->fabe", half_low, turned, precision=HIGHEST)
    high_first = jnp.einsum("ai,fibe->fabe", half_high, turned, precision=HIGHEST)
    first_pass = jnp.where(quad_first, low_first, high_first)
    low_second = jnp.einsum("bj,faje->fabe", half_low, first_pass, precision=HIGHEST)
    high_second = jnp.einsum("bj,faje->fabe", half_high, first_pass, precision=HIGHEST)
    second_pass = jnp.where(quad_second, low_second, high_second)
    return jnp.where(hanging, second_pass, turned)


def cell_term(cube, weights, stiffness):
    first_axis = jnp.einsum("ai,ijke->ajke", stiffness, cube, precision=HIGHEST) * (
        weights[None, :, None, None] * weights[None, None, :, None]
    )
    second_axis = jnp.einsum("bj,ijke->ibke", stiffness, cube, precision=HIGHEST) * (
        weights[:, None, None, None] * weights[None, None, :, None]
    )
    third_axis = jnp.einsum("ck,ijke->ijce", stiffness, cube, precision=HIGHEST) * (
        weights[:, None, None, None] * weights[None, :, None, None]
    )
    return first_axis + second_axis + third_axis


def diag_pattern(tables):
    weights, stiffness, half_low, half_high = tables
    count = weights.shape[0]
    stiff_diag = jnp.diagonal(stiffness)
    cell_diag = (
        stiff_diag[:, None, None] * weights[None, :, None] * weights[None, None, :]
        + weights[:, None, None] * stiff_diag[None, :, None] * weights[None, None, :]
        + weights[:, None, None] * weights[None, :, None] * stiff_diag[None, None, :]
    )
    face_mass = PENALTY * weights[:, None] * weights[None, :]
    face_values = jnp.broadcast_to(face_mass[None, :, :, None], (6, count, count, 1))
    pattern = add_faces(cell_diag[:, :, :, None], face_values)
    return pattern.reshape(count * count * count)


def neighbour_traces(traces, face_source, send_list, fields):
    count = traces.shape[1]
    elements = traces.shape[3] // fields
    wide = lax.axis_size("wide")
    rows = fields * count * count
    local = (
        traces.reshape(6, count * count, fields, elements)
        .transpose(2, 1, 0, 3)
        .reshape(rows, 6 * elements)
    )
    picked = local[:, send_list[0]]
    outgoing = picked.T.reshape(3, lax.axis_size("narrow"), -1)
    swapped = lax.all_to_all(outgoing, "narrow", split_axis=1, concat_axis=1, tiled=True)
    up = [(i, i + 1) for i in range(wide - 1)]
    down = [(i + 1, i) for i in range(wide - 1)]
    before = lax.ppermute(swapped[2], "wide", up)
    after = lax.ppermute(swapped[0], "wide", down)
    incoming = jnp.stack([before, swapped[1], after])
    received = incoming.reshape(-1, rows).T
    pool = jnp.concatenate([local, received, jnp.zeros((rows, 1), jnp.float32)], axis=1)
    columns = jnp.where(face_source < 0, pool.shape[1] - 1, face_source).reshape(-1)
    gathered = pool[:, columns]
    return (
        gathered.reshape(fields, count * count, 6, elements)
        .transpose(2, 1, 0, 3)
        .reshape(6, count, count, fields * elements)
    )


def chebyshev_coefficients(estimate):
    lam_max = SAFETY * estimate
    lam_min = lam_max / RANGE_RATIO
    theta = (lam_max + lam_min) / 2.0
    delta = (lam_max - lam_min) / 2.0
    sigma = theta / delta
    rho_now = 1.0 / sigma
    zero = jnp.zeros_like(estimate)
    direction = [1.0 / theta] + [zero] * (CHEB - 1)
    solution = list(direction)
    for iteration in range(CHEB - 1):
        scaled_resid = [1.0 - zero] + [-c for c in solution[:-1]]
        rho_new = 1.0 / (2.0 * sigma - rho_now)
        direction = [
            rho_new * rho_now * d + 2.0 * rho_new / delta * r
            for d, r in zip(direction, scaled_resid)
        ]
        solution = [s + d for s, d in zip(solution, direction)]
        rho_now = rho_new
    return solution


def body(rhs, levels, face_source, subface, orientation, send_list, parent, coarse_inverse):
    tables = gll_tables(NODES)
    weights, stiffness, half_low, half_high = tables
    count = NODES
    elements = rhs.shape[1]
    scale = jnp.exp2(-levels.astype(jnp.float32))
    inv_diag = 1.0 / (diag_pattern(tables)[:, None] * scale[None, :])
    face_mass = weights[:, None] * weights[None, :]

    def operator(fields):
        number = len(fields)
        field = jnp.concatenate(fields, axis=1) if number > 1 else fields[0]
        tiled_scale = jnp.tile(scale, number)
        cube = field.reshape(count, count, count, -1)
        traces = face_traces(cube)
        neighbour = orient_faces(
            neighbour_traces(traces, face_source, send_list, number),
            jnp.tile(orientation, (1, number)),
            jnp.tile(subface, (1, number)),
            half_low,
            half_high,
        )
        jumps = PENALTY * face_mass[None, :, :, None] * (traces - neighbour)
        total = add_faces(cell_term(cube, weights, stiffness), jumps)
        total = total.reshape(count * count * count, -1) * tiled_scale[None, :]
        return [total[:, k * elements:(k + 1) * elements] for k in range(number)]

    def paired_round(iteration, carry):
        power, previous, latest, krylov_stack, image_stack = carry
        both = operator([power, latest])
        latest = inv_diag * both[1]
        return (
            inv_diag * both[0],
            power,
            latest,
            lax.dynamic_update_index_in_dim(krylov_stack, latest, iteration, 0),
            lax.dynamic_update_index_in_dim(image_stack, both[1], iteration, 0),
        )

    start = inv_diag * rhs
    history = jnp.zeros((POWER,) + rhs.shape, rhs.dtype)
    power, previous, latest, krylov_stack, image_stack = lax.fori_loop(
        0, POWER, paired_round, (rhs, rhs, start, history, history)
    )
    krylov = [start] + [krylov_stack[j] for j in range(POWER)]
    images = [image_stack[j] for j in range(POWER)] + [operator([latest])[0]]

    mass = (weights[:, None, None] * weights[None, :, None] * weights[None, None, :]).reshape(
        count * count * count, 1
    )
    cells = coarse_inverse.shape[1]
    element_mass = jnp.stack([jnp.sum(mass * v, axis=0) for v in [rhs] + images], axis=1) / 8.0
    partial = jax.ops.segment_sum(element_mass, parent[0], num_segments=cells)
    norms = jnp.stack([jnp.sum(power * power), jnp.sum(previous * previous)])
    block = lax.psum(jnp.concatenate([norms, partial.reshape(-1)]), "narrow")
    wide = lax.axis_size("wide")
    spread = jnp.broadcast_to(block[None, :2], (wide, 2))
    norms = jnp.sum(lax.all_to_all(spread, "wide", 0, 0, tiled=True), axis=0)
    restricted = block[2:].reshape(cells, len(images) + 1)

    estimate = jnp.sqrt(norms[0] / norms[1])
    coefficients = chebyshev_coefficients(estimate)
    solution = coefficients[0] * krylov[0]
    applied = coefficients[0] * images[0]
    coarse_res = restricted[:, 0] - coefficients[0] * restricted[:, 1]
    for j in range(1, CHEB):
        solution = solution + coefficients[j] * krylov[j]
        applied = applied + coefficients[j] * images[j]
        coarse_res = coarse_res - coefficients[j] * restricted[:, j + 1]
    residual = rhs - applied
    coarse_cor = jnp.dot(coarse_inverse[0], coarse_res, precision=HIGHEST)
    corrected = solution + coarse_cor[parent[0]][None, :]
    return (corrected, residual)


def solution(mesh):
    in_specs = (
        P(None, ("wide", "narrow")),
        P(("wide", "narrow")),
        P(None, ("wide", "narrow")),
        P(None, ("wide", "narrow")),
        P(None, ("wide", "narrow")),
        P(("wide", "narrow"), None),
        P("wide", "narrow"),
        P("wide", None, None),
    )
    out_specs = (P(None, ("wide", "narrow")), P(None, ("wide", "narrow")))
    return jax.shard_map(body, mesh=mesh, in_specs=in_specs, out_specs=out_specs, check_vma=False)
```

profile of v0, /device:TPU:1, one launch (start us, length us, event | category | flops | bytes accessed | tf_op | source)
XLA Modules:
  0.0 197.1 jit_solution(17508117177648003702)
XLA Ops:
  5.8 107.4 %while.27 = (s32[]{:T(128)}, f32[512,128]{1,0:T(8,128)S(1)}, f32[512,128]{1,0:T(8,128)}, f32[512,128]{1,0:T(8,128)S(1)}, f32[3,512,128]{2,1,0:T(8,128)}, /*index...) while((s32[]{:T(128)}, f32[512,128]{1,0:T(8,128)S(1)}, ...), condition=%wide.region_1.2_spmd.clone.clone.clone, body=%wide.region_0.1_spmd.sunk.clone.clone.clone.sunk | while | flops 79930784 | bytes 39209528 | solution.py:228
  7.4 1.6 gather_fusion
  10.1 4.8 %all-to-all-start = ((f32[3,4,6144]{2,0,1:T(4,128)}), f32[3,4,6144]{2,0,1:T(4,128)S(1)}, u32[]{:S(2)}, u32[]{:S(2)}) async-start(f32[3,4,6144]{2,0,1:T(4,128)} %copy.623), calls=%async_computation | async-start | bytes 786432 | tf_op jit(solution)/shard_map/while/body/eval_jaxpr/all_to_all | solution.py:148
  18.2 3.0 %all-to-all-done = f32[3,4,6144]{2,0,1:T(4,128)S(1)} async-done(((f32[3,4,6144]{2,0,1:T(4,128)}), f32[3,4,6144]{2,0,1:T(4,128)S(1)}, u32[]{:S(2)}, u32[]{:S(2)}) %all-to-all-start) | async-done | bytes 294944 | tf_op jit(solution)/shard_map/while/body/eval_jaxpr/all_to_all | solution.py:148
  21.5 8.5 %collective-permute-start = (f32[4,6144]{1,0:T(4,128)S(1)}, f32[4,6144]{1,0:T(4,128)S(1)}, u32[]{:S(2)}, u32[]{:S(2)}) collective-permute-start(f32[4,6144]{1,0:T(4,128)S(1)} %bitcast.507), channel_id=1, source_target_pairs={{4,0},{8,4},{12,8},{16,12},{20,16},{24,20},{28,24},{32,28},{36,32}... | collective-permute-start | bytes 294920 | tf_op jit(solution)/shard_map/while/body/eval_jaxpr/ppermute | solution.py:152
  30.1 1.9 collective-permute-start.1
  41.6 1.7 fusion.201
  48.8 3.5 %all-to-all-start = ((f32[3,4,6144]{2,0,1:T(4,128)}), f32[3,4,6144]{2,0,1:T(4,128)S(1)}, u32[]{:S(2)}, u32[]{:S(2)}) async-start(f32[3,4,6144]{2,0,1:T(4,128)} %copy.623), calls=%async_computation | async-start | bytes 786432 | tf_op jit(solution)/shard_map/while/body/eval_jaxpr/all_to_all | solution.py:148
  55.5 5.1 %all-to-all-done = f32[3,4,6144]{2,0,1:T(4,128)S(1)} async-done(((f32[3,4,6144]{2,0,1:T(4,128)}), f32[3,4,6144]{2,0,1:T(4,128)S(1)}, u32[]{:S(2)}, u32[]{:S(2)}) %all-to-all-start) | async-done | bytes 294944 | tf_op jit(solution)/shard_map/while/body/eval_jaxpr/all_to_all | solution.py:148
  60.9 2.6 %collective-permute-start = (f32[4,6144]{1,0:T(4,128)S(1)}, f32[4,6144]{1,0:T(4,128)S(1)}, u32[]{:S(2)}, u32[]{:S(2)}) collective-permute-start(f32[4,6144]{1,0:T(4,128)S(1)} %bitcast.507), channel_id=1, source_target_pairs={{4,0},{8,4},{12,8},{16,12},{20,16},{24,20},{28,24},{32,28},{36,32}... | collective-permute-start | bytes 294920 | tf_op jit(solution)/shard_map/while/body/eval_jaxpr/ppermute | solution.py:152
  63.5 3.0 %collective-permute-start.1 = (f32[4,6144]{1,0:T(4,128)S(1)}, f32[4,6144]{1,0:T(4,128)S(1)}, u32[]{:S(2)}, u32[]{:S(2)}) collective-permute-start(f32[4,6144]{1,0:T(4,128)S(1)} %bitcast.508), channel_id=1, source_target_pairs={{0,4},{4,8},{8,12},{12,16},{16,20},{20,24},{24,28},{28,32},{32,36}... | collective-permute-start | bytes 294920 | tf_op jit(solution)/shard_map/while/body/eval_jaxpr/ppermute | solution.py:151
  76.1 1.7 fusion.201
  83.3 3.5 %all-to-all-start = ((f32[3,4,6144]{2,0,1:T(4,128)}), f32[3,4,6144]{2,0,1:T(4,128)S(1)}, u32[]{:S(2)}, u32[]{:S(2)}) async-start(f32[3,4,6144]{2,0,1:T(4,128)} %copy.623), calls=%async_computation | async-start | bytes 786432 | tf_op jit(solution)/shard_map/while/body/eval_jaxpr/all_to_all | solution.py:148
  90.0 4.3 %all-to-all-done = f32[3,4,6144]{2,0,1:T(4,128)S(1)} async-done(((f32[3,4,6144]{2,0,1:T(4,128)}), f32[3,4,6144]{2,0,1:T(4,128)S(1)}, u32[]{:S(2)}, u32[]{:S(2)}) %all-to-all-start) | async-done | bytes 294944 | tf_op jit(solution)/shard_map/while/body/eval_jaxpr/all_to_all | solution.py:148
  94.6 1.9 collective-permute-start
  96.5 4.2 %collective-permute-start.1 = (f32[4,6144]{1,0:T(4,128)S(1)}, f32[4,6144]{1,0:T(4,128)S(1)}, u32[]{:S(2)}, u32[]{:S(2)}) collective-permute-start(f32[4,6144]{1,0:T(4,128)S(1)} %bitcast.508), channel_id=1, source_target_pairs={{0,4},{4,8},{8,12},{12,16},{16,20},{20,24},{24,28},{28,32},{32,36}... | collective-permute-start | bytes 294920 | tf_op jit(solution)/shard_map/while/body/eval_jaxpr/ppermute | solution.py:151
  110.3 1.7 fusion.201
  116.1 3.5 %all-to-all-start.1 = ((f32[3,4,3072]{2,0,1:T(4,128)}), f32[3,4,3072]{2,0,1:T(4,128)S(1)}, u32[]{:S(2)}, u32[]{:S(2)}) async-start(f32[3,4,3072]{2,0,1:T(4,128)} %copy.404), calls=%async_computation.1 | async-start | bytes 393216 | tf_op jit(solution)/shard_map/all_to_all | solution.py:148
  124.8 5.4 %collective-permute-start.2 = (f32[4,3072]{1,0:T(4,128)S(1)}, f32[4,3072]{1,0:T(4,128)S(1)}, u32[]{:S(2)}, u32[]{:S(2)}) collective-permute-start(f32[4,3072]{1,0:T(4,128)S(1)} %bitcast.519), channel_id=1, source_target_pairs={{0,4},{4,8},{8,12},{12,16},{16,20},{20,24},{24,28},{28,32},{32,36}... | collective-permute-start | bytes 147464 | tf_op jit(solution)/shard_map/ppermute | solution.py:151
  130.2 1.9 collective-permute-start.3
  132.4 3.2 %collective-permute-done.3 = f32[4,3072]{1,0:T(4,128)S(1)} collective-permute-done((f32[4,3072]{1,0:T(4,128)S(1)}, f32[4,3072]{1,0:T(4,128)S(1)}, u32[]{:S(2)}, u32[]{:S(2)}) %collective-permute-start.3) | collective-permute-done | bytes 49184 | tf_op jit(solution)/shard_map/ppermute | solution.py:152
  145.6 7.6 %psum.7 = f32[642]{0:T(1024)S(1)} all-reduce(f32[642]{0:T(1024)S(1)} %pad_maximum_fusion.2), channel_id=1, replica_groups=mesh['wide'=128,'narrow'=4] {'narrow'}, use_global_device_ids=true, to_apply=%region_10.11 | all-reduce | flops 642 | bytes 5136 | tf_op jit(solution)/shard_map/psum | solution.py:241
  154.0 22.4 %all-to-all-start.2 = ((f32[128,1,2]{2,1,0:T(1,128)}), f32[128,1,2]{2,1,0:T(1,128)S(1)}, u32[]{:S(2)}, u32[]{:S(2)}) async-start(f32[128,1,2]{2,1,0:T(1,128)} %broadcast_in_dim.295), calls=%async_computation.2 | async-start | bytes 131072 | tf_op jit(solution)/shard_map/all_to_all | solution.py:244
  177.2 14.2 %all-to-all-done.2 = f32[128,1,2]{2,1,0:T(1,128)S(1)} async-done(((f32[128,1,2]{2,1,0:T(1,128)}), f32[128,1,2]{2,1,0:T(1,128)S(1)}, u32[]{:S(2)}, u32[]{:S(2)}) %all-to-all-start.2) | async-done | bytes 1056 | tf_op jit(solution)/shard_map/all_to_all | solution.py:244
  (395 shorter events, 81.4 us)
Async XLA Ops:
  0.6 194.1 %copy-start = (f32[1,128,128]{2,1,0:T(8,128)S(1)}, f32[1,128,128]{2,1,0:T(8,128)}, u32[]{:S(2)}) copy-start(f32[1,128,128]{2,1,0:T(8,128)} %param.21) | copy-start | bytes 196612
  0.7 2.7 %copy-start.21 = (f32[8]{0:T(128)}, f32[8]{0:T(128)S(1)}, u32[]{:S(2)}) copy-start(f32[8]{0:T(128)S(1)} %get-tuple-element.650) | copy-start | bytes 100
  0.7 2.6 %copy-start.23 = (f32[8]{0:T(128)}, f32[8]{0:T(128)S(1)}, u32[]{:S(2)}) copy-start(f32[8]{0:T(128)S(1)} %get-tuple-element.651) | copy-start | bytes 100
  10.1 11.1 %all-to-all-start = ((f32[3,4,6144]{2,0,1:T(4,128)}), f32[3,4,6144]{2,0,1:T(4,128)S(1)}, u32[]{:S(2)}, u32[]{:S(2)}) async-start(f32[3,4,6144]{2,0,1:T(4,128)} %copy.623), calls=%async_computation | async-start | bytes 786432 | tf_op jit(solution)/shard_map/while/body/eval_jaxpr/all_to_all | solution.py:148
  21.5 10.6 %collective-permute-start = (f32[4,6144]{1,0:T(4,128)S(1)}, f32[4,6144]{1,0:T(4,128)S(1)}, u32[]{:S(2)}, u32[]{:S(2)}) collective-permute-start(f32[4,6144]{1,0:T(4,128)S(1)} %bitcast.507), channel_id=1, source_target_pairs={{4,0},{8,4},{12,8},{16,12},{20,16},{24,20},{28,24},{32,28},{36,32}... | collective-permute-start | bytes 294920 | tf_op jit(solution)/shard_map/while/body/eval_jaxpr/ppermute | solution.py:152
  30.1 3.5 %collective-permute-start.1 = (f32[4,6144]{1,0:T(4,128)S(1)}, f32[4,6144]{1,0:T(4,128)S(1)}, u32[]{:S(2)}, u32[]{:S(2)}) collective-permute-start(f32[4,6144]{1,0:T(4,128)S(1)} %bitcast.508), channel_id=1, source_target_pairs={{0,4},{4,8},{8,12},{12,16},{16,20},{20,24},{24,28},{28,32},{32,36}... | collective-permute-start | bytes 294920 | tf_op jit(solution)/shard_map/while/body/eval_jaxpr/ppermute | solution.py:151
  39.8 1.0 copy-start.5
  48.8 11.8 %all-to-all-start = ((f32[3,4,6144]{2,0,1:T(4,128)}), f32[3,4,6144]{2,0,1:T(4,128)S(1)}, u32[]{:S(2)}, u32[]{:S(2)}) async-start(f32[3,4,6144]{2,0,1:T(4,128)} %copy.623), calls=%async_computation | async-start | bytes 786432 | tf_op jit(solution)/shard_map/while/body/eval_jaxpr/all_to_all | solution.py:148
  60.9 5.9 %collective-permute-start = (f32[4,6144]{1,0:T(4,128)S(1)}, f32[4,6144]{1,0:T(4,128)S(1)}, u32[]{:S(2)}, u32[]{:S(2)}) collective-permute-start(f32[4,6144]{1,0:T(4,128)S(1)} %bitcast.507), channel_id=1, source_target_pairs={{4,0},{8,4},{12,8},{16,12},{20,16},{24,20},{28,24},{32,28},{36,32}... | collective-permute-start | bytes 294920 | tf_op jit(solution)/shard_map/while/body/eval_jaxpr/ppermute | solution.py:152
  63.5 4.6 %collective-permute-start.1 = (f32[4,6144]{1,0:T(4,128)S(1)}, f32[4,6144]{1,0:T(4,128)S(1)}, u32[]{:S(2)}, u32[]{:S(2)}) collective-permute-start(f32[4,6144]{1,0:T(4,128)S(1)} %bitcast.508), channel_id=1, source_target_pairs={{0,4},{4,8},{8,12},{12,16},{16,20},{20,24},{24,28},{28,32},{32,36}... | collective-permute-start | bytes 294920 | tf_op jit(solution)/shard_map/while/body/eval_jaxpr/ppermute | solution.py:151
  74.3 1.0 copy-start.5
  83.3 11.0 %all-to-all-start = ((f32[3,4,6144]{2,0,1:T(4,128)}), f32[3,4,6144]{2,0,1:T(4,128)S(1)}, u32[]{:S(2)}, u32[]{:S(2)}) async-start(f32[3,4,6144]{2,0,1:T(4,128)} %copy.623), calls=%async_computation | async-start | bytes 786432 | tf_op jit(solution)/shard_map/while/body/eval_jaxpr/all_to_all | solution.py:148
  94.6 6.5 %collective-permute-start = (f32[4,6144]{1,0:T(4,128)S(1)}, f32[4,6144]{1,0:T(4,128)S(1)}, u32[]{:S(2)}, u32[]{:S(2)}) collective-permute-start(f32[4,6144]{1,0:T(4,128)S(1)} %bitcast.507), channel_id=1, source_target_pairs={{4,0},{8,4},{12,8},{16,12},{20,16},{24,20},{28,24},{32,28},{36,32}... | collective-permute-start | bytes 294920 | tf_op jit(solution)/shard_map/while/body/eval_jaxpr/ppermute | solution.py:152
  96.5 5.8 %collective-permute-start.1 = (f32[4,6144]{1,0:T(4,128)S(1)}, f32[4,6144]{1,0:T(4,128)S(1)}, u32[]{:S(2)}, u32[]{:S(2)}) collective-permute-start(f32[4,6144]{1,0:T(4,128)S(1)} %bitcast.508), channel_id=1, source_target_pairs={{0,4},{4,8},{8,12},{12,16},{16,20},{20,24},{24,28},{28,32},{32,36}... | collective-permute-start | bytes 294920 | tf_op jit(solution)/shard_map/while/body/eval_jaxpr/ppermute | solution.py:151
  108.5 1.0 copy-start.5
  115.1 6.7 %copy-start.31 = (s32[1,128]{1,0:T(1,128)S(1)}, s32[1,128]{1,0:T(1,128)}, u32[]{:S(2)}) copy-start(s32[1,128]{1,0:T(1,128)} %param.20) | copy-start | bytes 1540
  116.1 8.5 %all-to-all-start.1 = ((f32[3,4,3072]{2,0,1:T(4,128)}), f32[3,4,3072]{2,0,1:T(4,128)S(1)}, u32[]{:S(2)}, u32[]{:S(2)}) async-start(f32[3,4,3072]{2,0,1:T(4,128)} %copy.404), calls=%async_computation.1 | async-start | bytes 393216 | tf_op jit(solution)/shard_map/all_to_all | solution.py:148
  119.7 3.0 %copy-start.8 = (f32[512,128]{1,0:T(8,128)S(1)}, f32[512,128]{1,0:T(8,128)}, u32[]{:S(2)}) copy-start(f32[512,128]{1,0:T(8,128)} %get-tuple-element.448) | copy-start | bytes 786436
  120.8 2.6 %copy-start.6 = (f32[3,512,128]{2,1,0:T(8,128)S(1)}, f32[3,512,128]{2,1,0:T(8,128)}, u32[]{:S(2)}) copy-start(f32[3,512,128]{2,1,0:T(8,128)} %get-tuple-element.449) | copy-start | bytes 2359300
  124.8 7.6 %collective-permute-start.2 = (f32[4,3072]{1,0:T(4,128)S(1)}, f32[4,3072]{1,0:T(4,128)S(1)}, u32[]{:S(2)}, u32[]{:S(2)}) collective-permute-start(f32[4,3072]{1,0:T(4,128)S(1)} %bitcast.519), channel_id=1, source_target_pairs={{0,4},{4,8},{8,12},{12,16},{16,20},{20,24},{24,28},{28,32},{32,36}... | collective-permute-start | bytes 147464 | tf_op jit(solution)/shard_map/ppermute | solution.py:151
  130.2 5.4 %collective-permute-start.3 = (f32[4,3072]{1,0:T(4,128)S(1)}, f32[4,3072]{1,0:T(4,128)S(1)}, u32[]{:S(2)}, u32[]{:S(2)}) collective-permute-start(f32[4,3072]{1,0:T(4,128)S(1)} %bitcast.520), channel_id=1, source_target_pairs={{4,0},{8,4},{12,8},{16,12},{20,16},{24,20},{28,24},{32,28},{36,32}... | collective-permute-start | bytes 147464 | tf_op jit(solution)/shard_map/ppermute | solution.py:152
  139.9 1.0 copy-start.17
  154.0 37.4 %all-to-all-start.2 = ((f32[128,1,2]{2,1,0:T(1,128)}), f32[128,1,2]{2,1,0:T(1,128)S(1)}, u32[]{:S(2)}, u32[]{:S(2)}) async-start(f32[128,1,2]{2,1,0:T(1,128)} %broadcast_in_dim.295), calls=%async_computation.2 | async-start | bytes 131072 | tf_op jit(solution)/shard_map/all_to_all | solution.py:244
  193.9 2.3 %copy-start.9 = (f32[3,512,128]{2,1,0:T(8,128)S(1)}, f32[3,512,128]{2,1,0:T(8,128)}, u32[]{:S(2)}) copy-start(f32[3,512,128]{2,1,0:T(8,128)} %get-tuple-element.451) | copy-start | bytes 2359300
  (25 other events, 20.5 us)
where the time goes:
time: 198 us; the launch traced here: 197 us
  starting transfers between devices  67.1 us (34%)
  local copies, waits for them, and re-layouts  46.7 us (24%)
  waiting for transfers between devices  34.8 us (18%)
  matrix products  20 us (10%)
  other arithmetic  16.1 us (8%)
  blocking collectives  7.61 us (4%)
  between operations  3.07 us (2%)
    all_to_all x1, starting transfers between devices, body(): norms = jnp.sum(lax.all_to_all(spread, 'wide', 0, 0, tiled=True), axis=0)  22.4 us
    all_to_all x4, starting transfers between devices, neighbour_traces(): lax.all_to_all(outgoing, 'narrow', split_axis=1, concat_axis=1, tiled=True)  15.3 us
    ppermute x4, starting transfers between devices, neighbour_traces(): after = lax.ppermute(swapped[0], 'wide', down)  14.9 us
    ppermute x4, starting transfers between devices, neighbour_traces(): before = lax.ppermute(swapped[2], 'wide', up)  14.4 us
    all_to_all x1, waiting for transfers between devices, body(): norms = jnp.sum(lax.all_to_all(spread, 'wide', 0, 0, tiled=True), axis=0)  14.2 us
    all_to_all x4, waiting for transfers between devices, neighbour_traces(): lax.all_to_all(outgoing, 'narrow', split_axis=1, concat_axis=1, tiled=True)  12.8 us
    psum x1, blocking collectives, body(): block = lax.psum(jnp.concatenate([norms, partial.reshape(-1)]), 'narrow')  7.61 us
    while x69, local copies, waits for them, and re-layouts  6.97 us
  transfers between devices with their start and end apart: 13, of which 11 were waited for; matrix products, arithmetic and copies ran while one was open for 6% of the time, Pallas kernels for 0%

commit v1 on v0

--- a/solution.py
+++ b/solution.py
@@ -238,7 +238,10 @@
     element_mass = jnp.stack([jnp.sum(mass * v, axis=0) for v in [rhs] + images], axis=1) / 8.0
     partial = jax.ops.segment_sum(element_mass, parent[0], num_segments=cells)
     norms = jnp.stack([jnp.sum(power * power), jnp.sum(previous * previous)])
-    block = lax.psum(jnp.concatenate([norms, partial.reshape(-1)]), "narrow")
+    narrow = lax.axis_size("narrow")
+    local_block = jnp.concatenate([norms, partial.reshape(-1)])
+    shared = jnp.broadcast_to(local_block[None], (narrow,) + local_block.shape)
+    block = jnp.sum(lax.all_to_all(shared, "narrow", 0, 0, tiled=True), axis=0)
     wide = lax.axis_size("wide")
     spread = jnp.broadcast_to(block[None, :2], (wide, 2))
     norms = jnp.sum(lax.all_to_all(spread, "wide", 0, 0, tiled=True), axis=0)

time: 198 us -> 198 us (level)
  blocking collectives: 7.61 us -> 0 us
  waiting for transfers between devices: 34.8 us -> 39 us
  starting transfers between devices: 67.1 us -> 69.8 us
    psum x1 -> x0, blocking collectives: 7.61 us -> none  [body(): block = lax.psum(jnp.concatenate([norms, partial.reshape(-1)]), 'narrow')]
    all_to_all x0 -> x1, waiting for transfers between devices: none -> 4.11 us  [body(): block = jnp.sum(lax.all_to_all(shared, 'narrow', 0, 0, tiled=True), axis=0)]
    all_to_all x0 -> x1, starting transfers between devices: none -> 3.25 us  [body(): block = jnp.sum(lax.all_to_all(shared, 'narrow', 0, 0, tiled=True), axis=0)]
  transfers between devices with their start and end apart: 13 -> 14, of which waited for: 11 -> 12; matrix products, arithmetic and copies ran while one was open for 6% -> 6% of each run, Pallas kernels for 0% -> 0%
where the time goes in v1:
time: 198 us; the launch traced here: 197 us
  starting transfers between devices  69.8 us (35%)
  local copies, waits for them, and re-layouts  47.3 us (24%)
  waiting for transfers between devices  39 us (20%)
  matrix products  20 us (10%)
  other arithmetic  16.2 us (8%)
  between operations  3.09 us (2%)
    all_to_all x1, starting transfers between devices, body(): norms = jnp.sum(lax.all_to_all(spread, 'wide', 0, 0, tiled=True), axis=0)  21.8 us
    all_to_all x4, starting transfers between devices, neighbour_traces(): lax.all_to_all(outgoing, 'narrow', split_axis=1, concat_axis=1, tiled=True)  15.3 us
    ppermute x4, starting transfers between devices, neighbour_traces(): after = lax.ppermute(swapped[0], 'wide', down)  14.9 us
    ppermute x4, starting transfers between devices, neighbour_traces(): before = lax.ppermute(swapped[2], 'wide', up)  14.4 us
    all_to_all x1, waiting for transfers between devices, body(): norms = jnp.sum(lax.all_to_all(spread, 'wide', 0, 0, tiled=True), axis=0)  14.3 us
    all_to_all x4, waiting for transfers between devices, neighbour_traces(): lax.all_to_all(outgoing, 'narrow', split_axis=1, concat_axis=1, tiled=True)  12.8 us
    while x69, local copies, waits for them, and re-layouts  6.94 us
    gather x7, local copies, waits for them, and re-layouts, neighbour_traces(): gathered = pool[:, columns]  6.78 us
  transfers between devices with their start and end apart: 14, of which 12 were waited for; matrix products, arithmetic and copies ran while one was open for 6% of the time, Pallas kernels for 0%

profile of v1, /device:TPU:1, one launch (start us, length us, event | category | flops | bytes accessed | tf_op | source)
XLA Modules:
  0.0 197.0 jit_solution(11984164160698627256)
XLA Ops:
  5.8 107.4 %while.27 = (s32[]{:T(128)}, f32[512,128]{1,0:T(8,128)S(1)}, f32[512,128]{1,0:T(8,128)}, f32[512,128]{1,0:T(8,128)S(1)}, f32[3,512,128]{2,1,0:T(8,128)}, /*index...) while((s32[]{:T(128)}, f32[512,128]{1,0:T(8,128)S(1)}, ...), condition=%wide.region_1.2_spmd.clone.clone.clone, body=%wide.region_0.1_spmd.sunk.clone.clone.clone.sunk | while | flops 79930784 | bytes 39209528 | solution.py:228
  10.1 4.8 %all-to-all-start = ((f32[3,4,6144]{2,0,1:T(4,128)}), f32[3,4,6144]{2,0,1:T(4,128)S(1)}, u32[]{:S(2)}, u32[]{:S(2)}) async-start(f32[3,4,6144]{2,0,1:T(4,128)} %copy.628), calls=%async_computation | async-start | bytes 786432 | tf_op jit(solution)/shard_map/while/body/eval_jaxpr/all_to_all | solution.py:148
  18.2 3.0 %all-to-all-done = f32[3,4,6144]{2,0,1:T(4,128)S(1)} async-done(((f32[3,4,6144]{2,0,1:T(4,128)}), f32[3,4,6144]{2,0,1:T(4,128)S(1)}, u32[]{:S(2)}, u32[]{:S(2)}) %all-to-all-start) | async-done | bytes 294944 | tf_op jit(solution)/shard_map/while/body/eval_jaxpr/all_to_all | solution.py:148
  21.5 8.5 %collective-permute-start = (f32[4,6144]{1,0:T(4,128)S(1)}, f32[4,6144]{1,0:T(4,128)S(1)}, u32[]{:S(2)}, u32[]{:S(2)}) collective-permute-start(f32[4,6144]{1,0:T(4,128)S(1)} %bitcast.507), channel_id=1, source_target_pairs={{4,0},{8,4},{12,8},{16,12},{20,16},{24,20},{28,24},{32,28},{36,32}... | collective-permute-start | bytes 294920 | tf_op jit(solution)/shard_map/while/body/eval_jaxpr/ppermute | solution.py:152
  30.1 1.9 collective-permute-start.1
  41.6 1.7 fusion.201
  48.8 3.5 %all-to-all-start = ((f32[3,4,6144]{2,0,1:T(4,128)}), f32[3,4,6144]{2,0,1:T(4,128)S(1)}, u32[]{:S(2)}, u32[]{:S(2)}) async-start(f32[3,4,6144]{2,0,1:T(4,128)} %copy.628), calls=%async_computation | async-start | bytes 786432 | tf_op jit(solution)/shard_map/while/body/eval_jaxpr/all_to_all | solution.py:148
  55.5 5.1 %all-to-all-done = f32[3,4,6144]{2,0,1:T(4,128)S(1)} async-done(((f32[3,4,6144]{2,0,1:T(4,128)}), f32[3,4,6144]{2,0,1:T(4,128)S(1)}, u32[]{:S(2)}, u32[]{:S(2)}) %all-to-all-start) | async-done | bytes 294944 | tf_op jit(solution)/shard_map/while/body/eval_jaxpr/all_to_all | solution.py:148
  60.9 2.6 %collective-permute-start = (f32[4,6144]{1,0:T(4,128)S(1)}, f32[4,6144]{1,0:T(4,128)S(1)}, u32[]{:S(2)}, u32[]{:S(2)}) collective-permute-start(f32[4,6144]{1,0:T(4,128)S(1)} %bitcast.507), channel_id=1, source_target_pairs={{4,0},{8,4},{12,8},{16,12},{20,16},{24,20},{28,24},{32,28},{36,32}... | collective-permute-start | bytes 294920 | tf_op jit(solution)/shard_map/while/body/eval_jaxpr/ppermute | solution.py:152
  63.5 3.0 %collective-permute-start.1 = (f32[4,6144]{1,0:T(4,128)S(1)}, f32[4,6144]{1,0:T(4,128)S(1)}, u32[]{:S(2)}, u32[]{:S(2)}) collective-permute-start(f32[4,6144]{1,0:T(4,128)S(1)} %bitcast.508), channel_id=1, source_target_pairs={{0,4},{4,8},{8,12},{12,16},{16,20},{20,24},{24,28},{28,32},{32,36}... | collective-permute-start | bytes 294920 | tf_op jit(solution)/shard_map/while/body/eval_jaxpr/ppermute | solution.py:151
  76.1 1.7 fusion.201
  83.3 3.5 %all-to-all-start = ((f32[3,4,6144]{2,0,1:T(4,128)}), f32[3,4,6144]{2,0,1:T(4,128)S(1)}, u32[]{:S(2)}, u32[]{:S(2)}) async-start(f32[3,4,6144]{2,0,1:T(4,128)} %copy.628), calls=%async_computation | async-start | bytes 786432 | tf_op jit(solution)/shard_map/while/body/eval_jaxpr/all_to_all | solution.py:148
  90.0 4.3 %all-to-all-done = f32[3,4,6144]{2,0,1:T(4,128)S(1)} async-done(((f32[3,4,6144]{2,0,1:T(4,128)}), f32[3,4,6144]{2,0,1:T(4,128)S(1)}, u32[]{:S(2)}, u32[]{:S(2)}) %all-to-all-start) | async-done | bytes 294944 | tf_op jit(solution)/shard_map/while/body/eval_jaxpr/all_to_all | solution.py:148
  94.5 1.9 collective-permute-start
  96.5 4.2 %collective-permute-start.1 = (f32[4,6144]{1,0:T(4,128)S(1)}, f32[4,6144]{1,0:T(4,128)S(1)}, u32[]{:S(2)}, u32[]{:S(2)}) collective-permute-start(f32[4,6144]{1,0:T(4,128)S(1)} %bitcast.508), channel_id=1, source_target_pairs={{0,4},{4,8},{8,12},{12,16},{16,20},{20,24},{24,28},{28,32},{32,36}... | collective-permute-start | bytes 294920 | tf_op jit(solution)/shard_map/while/body/eval_jaxpr/ppermute | solution.py:151
  110.3 1.7 fusion.201
  116.1 3.5 %all-to-all-start.1 = ((f32[3,4,3072]{2,0,1:T(4,128)}), f32[3,4,3072]{2,0,1:T(4,128)S(1)}, u32[]{:S(2)}, u32[]{:S(2)}) async-start(f32[3,4,3072]{2,0,1:T(4,128)} %copy.405), calls=%async_computation.1 | async-start | bytes 393216 | tf_op jit(solution)/shard_map/all_to_all | solution.py:148
  124.9 5.3 %collective-permute-start.2 = (f32[4,3072]{1,0:T(4,128)S(1)}, f32[4,3072]{1,0:T(4,128)S(1)}, u32[]{:S(2)}, u32[]{:S(2)}) collective-permute-start(f32[4,3072]{1,0:T(4,128)S(1)} %bitcast.519), channel_id=1, source_target_pairs={{0,4},{4,8},{8,12},{12,16},{16,20},{20,24},{24,28},{28,32},{32,36}... | collective-permute-start | bytes 147464 | tf_op jit(solution)/shard_map/ppermute | solution.py:151
  130.2 1.9 collective-permute-start.3
  132.4 3.2 %collective-permute-done.3 = f32[4,3072]{1,0:T(4,128)S(1)} collective-permute-done((f32[4,3072]{1,0:T(4,128)S(1)}, f32[4,3072]{1,0:T(4,128)S(1)}, u32[]{:S(2)}, u32[]{:S(2)}) %collective-permute-start.3) | collective-permute-done | bytes 49184 | tf_op jit(solution)/shard_map/ppermute | solution.py:152
  146.3 3.3 %all-to-all-start.2 = ((f32[4,1,642]{2,1,0:T(1,128)}), f32[4,1,642]{2,1,0:T(1,128)S(1)}, u32[]{:S(2)}, u32[]{:S(2)}) async-start(f32[4,1,642]{2,1,0:T(1,128)} %broadcast_in_dim.301), calls=%async_computation.2 | async-start | bytes 24576 | tf_op jit(solution)/shard_map/all_to_all | solution.py:244
  149.6 4.1 %all-to-all-done.2 = f32[4,1,642]{2,1,0:T(1,128)S(1)} async-done(((f32[4,1,642]{2,1,0:T(1,128)}), f32[4,1,642]{2,1,0:T(1,128)S(1)}, u32[]{:S(2)}, u32[]{:S(2)}) %all-to-all-start.2) | async-done | bytes 10304 | tf_op jit(solution)/shard_map/all_to_all | solution.py:244
  154.5 21.8 %all-to-all-start.3 = ((f32[128,1,2]{2,1,0:T(1,128)}), f32[128,1,2]{2,1,0:T(1,128)S(1)}, u32[]{:S(2)}, u32[]{:S(2)}) async-start(f32[128,1,2]{2,1,0:T(1,128)} %broadcast_in_dim.302), calls=%async_computation.3 | async-start | bytes 131072 | tf_op jit(solution)/shard_map/all_to_all | solution.py:247
  177.1 14.3 %all-to-all-done.3 = f32[128,1,2]{2,1,0:T(1,128)S(1)} async-done(((f32[128,1,2]{2,1,0:T(1,128)}), f32[128,1,2]{2,1,0:T(1,128)S(1)}, u32[]{:S(2)}, u32[]{:S(2)}) %all-to-all-start.3) | async-done | bytes 1056 | tf_op jit(solution)/shard_map/all_to_all | solution.py:247
  (398 shorter events, 83.7 us)
Async XLA Ops:
  0.6 194.0 %copy-start = (f32[1,128,128]{2,1,0:T(8,128)S(1)}, f32[1,128,128]{2,1,0:T(8,128)}, u32[]{:S(2)}) copy-start(f32[1,128,128]{2,1,0:T(8,128)} %param.21) | copy-start | bytes 196612
  0.7 2.7 %copy-start.21 = (f32[8]{0:T(128)}, f32[8]{0:T(128)S(1)}, u32[]{:S(2)}) copy-start(f32[8]{0:T(128)S(1)} %get-tuple-element.650) | copy-start | bytes 100
  0.7 2.6 %copy-start.23 = (f32[8]{0:T(128)}, f32[8]{0:T(128)S(1)}, u32[]{:S(2)}) copy-start(f32[8]{0:T(128)S(1)} %get-tuple-element.651) | copy-start | bytes 100
  10.1 11.1 %all-to-all-start = ((f32[3,4,6144]{2,0,1:T(4,128)}), f32[3,4,6144]{2,0,1:T(4,128)S(1)}, u32[]{:S(2)}, u32[]{:S(2)}) async-start(f32[3,4,6144]{2,0,1:T(4,128)} %copy.628), calls=%async_computation | async-start | bytes 786432 | tf_op jit(solution)/shard_map/while/body/eval_jaxpr/all_to_all | solution.py:148
  21.5 10.6 %collective-permute-start = (f32[4,6144]{1,0:T(4,128)S(1)}, f32[4,6144]{1,0:T(4,128)S(1)}, u32[]{:S(2)}, u32[]{:S(2)}) collective-permute-start(f32[4,6144]{1,0:T(4,128)S(1)} %bitcast.507), channel_id=1, source_target_pairs={{4,0},{8,4},{12,8},{16,12},{20,16},{24,20},{28,24},{32,28},{36,32}... | collective-permute-start | bytes 294920 | tf_op jit(solution)/shard_map/while/body/eval_jaxpr/ppermute | solution.py:152
  30.1 3.5 %collective-permute-start.1 = (f32[4,6144]{1,0:T(4,128)S(1)}, f32[4,6144]{1,0:T(4,128)S(1)}, u32[]{:S(2)}, u32[]{:S(2)}) collective-permute-start(f32[4,6144]{1,0:T(4,128)S(1)} %bitcast.508), channel_id=1, source_target_pairs={{0,4},{4,8},{8,12},{12,16},{16,20},{20,24},{24,28},{28,32},{32,36}... | collective-permute-start | bytes 294920 | tf_op jit(solution)/shard_map/while/body/eval_jaxpr/ppermute | solution.py:151
  39.8 1.0 copy-start.5
  48.8 11.8 %all-to-all-start = ((f32[3,4,6144]{2,0,1:T(4,128)}), f32[3,4,6144]{2,0,1:T(4,128)S(1)}, u32[]{:S(2)}, u32[]{:S(2)}) async-start(f32[3,4,6144]{2,0,1:T(4,128)} %copy.628), calls=%async_computation | async-start | bytes 786432 | tf_op jit(solution)/shard_map/while/body/eval_jaxpr/all_to_all | solution.py:148
  60.9 5.9 %collective-permute-start = (f32[4,6144]{1,0:T(4,128)S(1)}, f32[4,6144]{1,0:T(4,128)S(1)}, u32[]{:S(2)}, u32[]{:S(2)}) collective-permute-start(f32[4,6144]{1,0:T(4,128)S(1)} %bitcast.507), channel_id=1, source_target_pairs={{4,0},{8,4},{12,8},{16,12},{20,16},{24,20},{28,24},{32,28},{36,32}... | collective-permute-start | bytes 294920 | tf_op jit(solution)/shard_map/while/body/eval_jaxpr/ppermute | solution.py:152
  63.5 4.6 %collective-permute-start.1 = (f32[4,6144]{1,0:T(4,128)S(1)}, f32[4,6144]{1,0:T(4,128)S(1)}, u32[]{:S(2)}, u32[]{:S(2)}) collective-permute-start(f32[4,6144]{1,0:T(4,128)S(1)} %bitcast.508), channel_id=1, source_target_pairs={{0,4},{4,8},{8,12},{12,16},{16,20},{20,24},{24,28},{28,32},{32,36}... | collective-permute-start | bytes 294920 | tf_op jit(solution)/shard_map/while/body/eval_jaxpr/ppermute | solution.py:151
  74.3 1.0 copy-start.5
  83.3 11.0 %all-to-all-start = ((f32[3,4,6144]{2,0,1:T(4,128)}), f32[3,4,6144]{2,0,1:T(4,128)S(1)}, u32[]{:S(2)}, u32[]{:S(2)}) async-start(f32[3,4,6144]{2,0,1:T(4,128)} %copy.628), calls=%async_computation | async-start | bytes 786432 | tf_op jit(solution)/shard_map/while/body/eval_jaxpr/all_to_all | solution.py:148
  94.5 6.5 %collective-permute-start = (f32[4,6144]{1,0:T(4,128)S(1)}, f32[4,6144]{1,0:T(4,128)S(1)}, u32[]{:S(2)}, u32[]{:S(2)}) collective-permute-start(f32[4,6144]{1,0:T(4,128)S(1)} %bitcast.507), channel_id=1, source_target_pairs={{4,0},{8,4},{12,8},{16,12},{20,16},{24,20},{28,24},{32,28},{36,32}... | collective-permute-start | bytes 294920 | tf_op jit(solution)/shard_map/while/body/eval_jaxpr/ppermute | solution.py:152
  96.5 5.8 %collective-permute-start.1 = (f32[4,6144]{1,0:T(4,128)S(1)}, f32[4,6144]{1,0:T(4,128)S(1)}, u32[]{:S(2)}, u32[]{:S(2)}) collective-permute-start(f32[4,6144]{1,0:T(4,128)S(1)} %bitcast.508), channel_id=1, source_target_pairs={{0,4},{4,8},{8,12},{12,16},{16,20},{20,24},{24,28},{28,32},{32,36}... | collective-permute-start | bytes 294920 | tf_op jit(solution)/shard_map/while/body/eval_jaxpr/ppermute | solution.py:151
  115.1 6.8 %copy-start.31 = (s32[1,128]{1,0:T(1,128)S(1)}, s32[1,128]{1,0:T(1,128)}, u32[]{:S(2)}) copy-start(s32[1,128]{1,0:T(1,128)} %param.20) | copy-start | bytes 1540
  116.1 8.5 %all-to-all-start.1 = ((f32[3,4,3072]{2,0,1:T(4,128)}), f32[3,4,3072]{2,0,1:T(4,128)S(1)}, u32[]{:S(2)}, u32[]{:S(2)}) async-start(f32[3,4,3072]{2,0,1:T(4,128)} %copy.405), calls=%async_computation.1 | async-start | bytes 393216 | tf_op jit(solution)/shard_map/all_to_all | solution.py:148
  119.7 3.0 %copy-start.8 = (f32[512,128]{1,0:T(8,128)S(1)}, f32[512,128]{1,0:T(8,128)}, u32[]{:S(2)}) copy-start(f32[512,128]{1,0:T(8,128)} %get-tuple-element.448) | copy-start | bytes 786436
  120.8 2.7 %copy-start.6 = (f32[3,512,128]{2,1,0:T(8,128)S(1)}, f32[3,512,128]{2,1,0:T(8,128)}, u32[]{:S(2)}) copy-start(f32[3,512,128]{2,1,0:T(8,128)} %get-tuple-element.449) | copy-start | bytes 2359300
  124.9 7.6 %collective-permute-start.2 = (f32[4,3072]{1,0:T(4,128)S(1)}, f32[4,3072]{1,0:T(4,128)S(1)}, u32[]{:S(2)}, u32[]{:S(2)}) collective-permute-start(f32[4,3072]{1,0:T(4,128)S(1)} %bitcast.519), channel_id=1, source_target_pairs={{0,4},{4,8},{8,12},{12,16},{16,20},{20,24},{24,28},{28,32},{32,36}... | collective-permute-start | bytes 147464 | tf_op jit(solution)/shard_map/ppermute | solution.py:151
  130.2 5.4 %collective-permute-start.3 = (f32[4,3072]{1,0:T(4,128)S(1)}, f32[4,3072]{1,0:T(4,128)S(1)}, u32[]{:S(2)}, u32[]{:S(2)}) collective-permute-start(f32[4,3072]{1,0:T(4,128)S(1)} %bitcast.520), channel_id=1, source_target_pairs={{4,0},{8,4},{12,8},{16,12},{20,16},{24,20},{28,24},{32,28},{36,32}... | collective-permute-start | bytes 147464 | tf_op jit(solution)/shard_map/ppermute | solution.py:152
  139.9 1.0 copy-start.17
  146.3 7.4 %all-to-all-start.2 = ((f32[4,1,642]{2,1,0:T(1,128)}), f32[4,1,642]{2,1,0:T(1,128)S(1)}, u32[]{:S(2)}, u32[]{:S(2)}) async-start(f32[4,1,642]{2,1,0:T(1,128)} %broadcast_in_dim.301), calls=%async_computation.2 | async-start | bytes 24576 | tf_op jit(solution)/shard_map/all_to_all | solution.py:244
  154.5 36.8 %all-to-all-start.3 = ((f32[128,1,2]{2,1,0:T(1,128)}), f32[128,1,2]{2,1,0:T(1,128)S(1)}, u32[]{:S(2)}, u32[]{:S(2)}) async-start(f32[128,1,2]{2,1,0:T(1,128)} %broadcast_in_dim.302), calls=%async_computation.3 | async-start | bytes 131072 | tf_op jit(solution)/shard_map/all_to_all | solution.py:247
  193.8 2.3 %copy-start.9 = (f32[3,512,128]{2,1,0:T(8,128)S(1)}, f32[3,512,128]{2,1,0:T(8,128)}, u32[]{:S(2)}) copy-start(f32[3,512,128]{2,1,0:T(8,128)} %get-tuple-element.451) | copy-start | bytes 2359300
  (26 other events, 21.5 us)

commit v2 on v1

--- a/solution.py
+++ b/solution.py
@@ -133,7 +133,7 @@
     return pattern.reshape(count * count * count)
 
 
-def neighbour_traces(traces, face_source, send_list, fields):
+def neighbour_traces(traces, face_source, send_list, fields, cover):
     count = traces.shape[1]
     elements = traces.shape[3] // fields
     wide = lax.axis_size("wide")
@@ -146,6 +146,7 @@
     picked = local[:, send_list[0]]
     outgoing = picked.T.reshape(3, lax.axis_size("narrow"), -1)
     swapped = lax.all_to_all(outgoing, "narrow", split_axis=1, concat_axis=1, tiled=True)
+    swapped, cover = lax.optimization_barrier((swapped, cover))
     up = [(i, i + 1) for i in range(wide - 1)]
     down = [(i + 1, i) for i in range(wide - 1)]
     before = lax.ppermute(swapped[2], "wide", up)
@@ -159,7 +160,7 @@
         gathered.reshape(fields, count * count, 6, elements)
         .transpose(2, 1, 0, 3)
         .reshape(6, count, count, fields * elements)
-    )
+    ), cover
 
 
 def chebyshev_coefficients(estimate):
@@ -199,15 +200,18 @@
         tiled_scale = jnp.tile(scale, number)
         cube = field.reshape(count, count, count, -1)
         traces = face_traces(cube)
+        gathered, cell = neighbour_traces(
+            traces, face_source, send_list, number, cell_term(cube, weights, stiffness)
+        )
         neighbour = orient_faces(
-            neighbour_traces(traces, face_source, send_list, number),
+            gathered,
             jnp.tile(orientation, (1, number)),
             jnp.tile(subface, (1, number)),
             half_low,
             half_high,
         )
         jumps = PENALTY * face_mass[None, :, :, None] * (traces - neighbour)
-        total = add_faces(cell_term(cube, weights, stiffness), jumps)
+        total = add_faces(cell, jumps)
         total = total.reshape(count * count * count, -1) * tiled_scale[None, :]
         return [total[:, k * elements:(k + 1) * elements] for k in range(number)]
 

time: 198 us -> 204 us (1.030)
  local copies, waits for them, and re-layouts: 47.3 us -> 59.4 us
  waiting for transfers between devices: 39 us -> 30.5 us
  starting transfers between devices: 69.8 us -> 72.9 us
    while x69 -> x87, local copies, waits for them, and re-layouts: 6.94 us -> 13.3 us
    all_to_all x4, waiting for transfers between devices: 12.8 us -> 6.8 us  [neighbour_traces(): lax.all_to_all(outgoing, 'narrow', split_axis=1, concat_axis=1, tiled=True)]
    unnamed x79 -> x83, local copies, waits for them, and re-layouts: 6.52 us -> 11.2 us
    ppermute x4, waiting for transfers between devices: 3.71 us -> 0.65 us  [neighbour_traces(): after = lax.ppermute(swapped[0], 'wide', down)]
    concatenate x4, other arithmetic: 3.84 us -> 0.96 us  [neighbour_traces(): jnp.concatenate([local, received, jnp.zeros((rows, 1), jnp.float32)], axi...]
    all_to_all x1, starting transfers between devices: 21.8 us -> 24.2 us  [body(): norms = jnp.sum(lax.all_to_all(spread, 'wide', 0, 0, tiled=True), axis=0)]
    reshape x4, local copies, waits for them, and re-layouts: 2.76 us -> 0.63 us  [neighbour_traces(): received = incoming.reshape(-1, rows).T]
  transfers between devices with their start and end apart: 14 -> 14, of which waited for: 12 -> 11; matrix products, arithmetic and copies ran while one was open for 6% -> 10% of each run, Pallas kernels for 0% -> 0%
where the time goes in v2:
time: 204 us; the launch traced here: 202 us
  starting transfers between devices  72.9 us (36%)
  local copies, waits for them, and re-layouts  59.4 us (29%)
  waiting for transfers between devices  30.5 us (15%)
  matrix products  18.7 us (9%)
  other arithmetic  16.3 us (8%)
  between operations  3.03 us (1%)
    all_to_all x1, starting transfers between devices, body(): norms = jnp.sum(lax.all_to_all(spread, 'wide', 0, 0, tiled=True), axis=0)  24.2 us
    all_to_all x4, starting transfers between devices, neighbour_traces(): lax.all_to_all(outgoing, 'narrow', split_axis=1, concat_axis=1, tiled=True)  15.9 us
    ppermute x4, starting transfers between devices, neighbour_traces(): after = lax.ppermute(swapped[0], 'wide', down)  14.9 us
    all_to_all x1, waiting for transfers between devices, body(): norms = jnp.sum(lax.all_to_all(spread, 'wide', 0, 0, tiled=True), axis=0)  14.5 us
    ppermute x4, starting transfers between devices, neighbour_traces(): before = lax.ppermute(swapped[2], 'wide', up)  13.4 us
    while x87, local copies, waits for them, and re-layouts  13.3 us
    unnamed x83, local copies, waits for them, and re-layouts  11.2 us
    all_to_all x4, waiting for transfers between devices, neighbour_traces(): lax.all_to_all(outgoing, 'narrow', split_axis=1, concat_axis=1, tiled=True)  6.8 us
  transfers between devices with their start and end apart: 14, of which 11 were waited for; matrix products, arithmetic and copies ran while one was open for 10% of the time, Pallas kernels for 0%

profile of v2, /device:TPU:1, one launch (start us, length us, event | category | flops | bytes accessed | tf_op | source)
XLA Modules:
  0.0 202.5 jit_solution(6497005565700767832)
XLA Ops:
  8.5 104.1 %while.27 = (s32[]{:T(128)}, f32[512,128]{1,0:T(8,128)S(1)}, f32[512,128]{1,0:T(8,128)}, f32[512,128]{1,0:T(8,128)S(1)}, f32[3,512,128]{2,1,0:T(8,128)}, /*index...) while((s32[]{:T(128)}, f32[512,128]{1,0:T(8,128)S(1)}, ...), condition=%wide.region_1.2_spmd.clone.clone.clone, body=%wide.region_0.1_spmd.sunk.clone.clone.clone.sunk | while | flops 79930784 | bytes 40470192 | solution.py:232
  10.7 1.6 gather_fusion
  13.4 4.8 %all-to-all-start = ((f32[3,4,6144]{2,0,1:T(4,128)}), f32[3,4,6144]{2,0,1:T(4,128)S(1)}, u32[]{:S(2)}, u32[]{:S(2)}) async-start(f32[3,4,6144]{2,0,1:T(4,128)} %copy.616), calls=%async_computation | async-start | bytes 786432 | tf_op jit(solution)/shard_map/while/body/eval_jaxpr/all_to_all | solution.py:148
  24.8 8.5 %collective-permute-start = (f32[4,6144]{1,0:T(4,128)S(1)}, f32[4,6144]{1,0:T(4,128)S(1)}, u32[]{:S(2)}, u32[]{:S(2)}) collective-permute-start(f32[4,6144]{1,0:T(4,128)S(1)} %bitcast.481), channel_id=1, source_target_pairs={{4,0},{8,4},{12,8},{16,12},{20,16},{24,20},{28,24},{32,28},{36,32}... | collective-permute-start | bytes 294920 | tf_op jit(solution)/shard_map/while/body/eval_jaxpr/ppermute | solution.py:153
  33.3 1.9 collective-permute-start.1
  35.3 1.6 collective-permute-done.1
  48.2 1.6 gather_fusion
  50.9 3.5 %all-to-all-start = ((f32[3,4,6144]{2,0,1:T(4,128)}), f32[3,4,6144]{2,0,1:T(4,128)S(1)}, u32[]{:S(2)}, u32[]{:S(2)}) async-start(f32[3,4,6144]{2,0,1:T(4,128)} %copy.616), calls=%async_computation | async-start | bytes 786432 | tf_op jit(solution)/shard_map/while/body/eval_jaxpr/all_to_all | solution.py:148
  59.5 3.3 %all-to-all-done = f32[3,4,6144]{2,0,1:T(4,128)S(1)} async-done(((f32[3,4,6144]{2,0,1:T(4,128)}), f32[3,4,6144]{2,0,1:T(4,128)S(1)}, u32[]{:S(2)}, u32[]{:S(2)}) %all-to-all-start) | async-done | bytes 294944 | tf_op jit(solution)/shard_map/while/body/eval_jaxpr/all_to_all | solution.py:148
  63.1 2.6 %collective-permute-start = (f32[4,6144]{1,0:T(4,128)S(1)}, f32[4,6144]{1,0:T(4,128)S(1)}, u32[]{:S(2)}, u32[]{:S(2)}) collective-permute-start(f32[4,6144]{1,0:T(4,128)S(1)} %bitcast.481), channel_id=1, source_target_pairs={{4,0},{8,4},{12,8},{16,12},{20,16},{24,20},{28,24},{32,28},{36,32}... | collective-permute-start | bytes 294920 | tf_op jit(solution)/shard_map/while/body/eval_jaxpr/ppermute | solution.py:153
  65.7 3.0 %collective-permute-start.1 = (f32[4,6144]{1,0:T(4,128)S(1)}, f32[4,6144]{1,0:T(4,128)S(1)}, u32[]{:S(2)}, u32[]{:S(2)}) collective-permute-start(f32[4,6144]{1,0:T(4,128)S(1)} %get-tuple-element.781), channel_id=1, source_target_pairs={{0,4},{4,8},{8,12},{12,16},{16,20},{20,24},{24,28},{28,32},{32,36}... | collective-permute-start | bytes 294920 | tf_op jit(solution)/shard_map/while/body/eval_jaxpr/ppermute | solution.py:152
  81.7 1.6 gather_fusion
  84.3 3.5 %all-to-all-start = ((f32[3,4,6144]{2,0,1:T(4,128)}), f32[3,4,6144]{2,0,1:T(4,128)S(1)}, u32[]{:S(2)}, u32[]{:S(2)}) async-start(f32[3,4,6144]{2,0,1:T(4,128)} %copy.616), calls=%async_computation | async-start | bytes 786432 | tf_op jit(solution)/shard_map/while/body/eval_jaxpr/all_to_all | solution.py:148
  92.9 2.4 %all-to-all-done = f32[3,4,6144]{2,0,1:T(4,128)S(1)} async-done(((f32[3,4,6144]{2,0,1:T(4,128)}), f32[3,4,6144]{2,0,1:T(4,128)S(1)}, u32[]{:S(2)}, u32[]{:S(2)}) %all-to-all-start) | async-done | bytes 294944 | tf_op jit(solution)/shard_map/while/body/eval_jaxpr/all_to_all | solution.py:148
  95.6 1.9 collective-permute-start
  97.6 4.2 %collective-permute-start.1 = (f32[4,6144]{1,0:T(4,128)S(1)}, f32[4,6144]{1,0:T(4,128)S(1)}, u32[]{:S(2)}, u32[]{:S(2)}) collective-permute-start(f32[4,6144]{1,0:T(4,128)S(1)} %get-tuple-element.781), channel_id=1, source_target_pairs={{0,4},{4,8},{8,12},{12,16},{16,20},{20,24},{24,28},{28,32},{32,36}... | collective-permute-start | bytes 294920 | tf_op jit(solution)/shard_map/while/body/eval_jaxpr/ppermute | solution.py:152
  113.4 1.6 gather_fusion.3
  116.0 4.2 %all-to-all-start.1 = ((f32[3,4,3072]{2,0,1:T(4,128)}), f32[3,4,3072]{2,0,1:T(4,128)}, u32[]{:S(2)}, u32[]{:S(2)}) async-start(f32[3,4,3072]{2,0,1:T(4,128)} %copy.398), calls=%async_computation.1 | async-start | bytes 393216 | tf_op jit(solution)/shard_map/all_to_all | solution.py:148
  129.7 1.9 collective-permute-start.3
  131.7 4.3 %collective-permute-start.2 = (f32[4,3072]{1,0:T(4,128)S(1)}, f32[4,3072]{1,0:T(4,128)S(1)}, u32[]{:S(2)}, u32[]{:S(2)}) collective-permute-start(f32[4,3072]{1,0:T(4,128)S(1)} %get-tuple-element.641), channel_id=1, source_target_pairs={{0,4},{4,8},{8,12},{12,16},{16,20},{20,24},{24,28},{28,32},{32,36}... | collective-permute-start | bytes 147464 | tf_op jit(solution)/shard_map/ppermute | solution.py:152
  147.0 4.5 %all-to-all-start.2 = ((f32[4,1,642]{2,1,0:T(1,128)}), f32[4,1,642]{2,1,0:T(1,128)S(1)}, u32[]{:S(2)}, u32[]{:S(2)}) async-start(f32[4,1,642]{2,1,0:T(1,128)} %broadcast_in_dim.301), calls=%async_computation.2 | async-start | bytes 24576 | tf_op jit(solution)/shard_map/all_to_all | solution.py:248
  151.6 4.1 %all-to-all-done.2 = f32[4,1,642]{2,1,0:T(1,128)S(1)} async-done(((f32[4,1,642]{2,1,0:T(1,128)}), f32[4,1,642]{2,1,0:T(1,128)S(1)}, u32[]{:S(2)}, u32[]{:S(2)}) %all-to-all-start.2) | async-done | bytes 10304 | tf_op jit(solution)/shard_map/all_to_all | solution.py:248
  157.7 24.2 %all-to-all-start.3 = ((f32[128,1,2]{2,1,0:T(1,128)}), f32[128,1,2]{2,1,0:T(1,128)S(1)}, u32[]{:S(2)}, u32[]{:S(2)}) async-start(f32[128,1,2]{2,1,0:T(1,128)} %broadcast_in_dim.302), calls=%async_computation.3 | async-start | bytes 131072 | tf_op jit(solution)/shard_map/all_to_all | solution.py:251
  182.4 14.5 %all-to-all-done.3 = f32[128,1,2]{2,1,0:T(1,128)S(1)} async-done(((f32[128,1,2]{2,1,0:T(1,128)}), f32[128,1,2]{2,1,0:T(1,128)S(1)}, u32[]{:S(2)}, u32[]{:S(2)}) %all-to-all-start.3) | async-done | bytes 1056 | tf_op jit(solution)/shard_map/all_to_all | solution.py:251
  (433 shorter events, 92.6 us)
Async XLA Ops:
  0.6 199.5 %copy-start = (f32[1,128,128]{2,1,0:T(8,128)S(1)}, f32[1,128,128]{2,1,0:T(8,128)}, u32[]{:S(2)}) copy-start(f32[1,128,128]{2,1,0:T(8,128)} %param.21) | copy-start | bytes 196612
  2.3 2.8 %copy-start.26 = (f32[8]{0:T(128)}, f32[8]{0:T(128)S(1)}, u32[]{:S(2)}) copy-start(f32[8]{0:T(128)S(1)} %get-tuple-element.662) | copy-start | bytes 100
  2.4 2.8 %copy-start.28 = (f32[8]{0:T(128)}, f32[8]{0:T(128)S(1)}, u32[]{:S(2)}) copy-start(f32[8]{0:T(128)S(1)} %get-tuple-element.663) | copy-start | bytes 100
  13.4 11.1 %all-to-all-start = ((f32[3,4,6144]{2,0,1:T(4,128)}), f32[3,4,6144]{2,0,1:T(4,128)S(1)}, u32[]{:S(2)}, u32[]{:S(2)}) async-start(f32[3,4,6144]{2,0,1:T(4,128)} %copy.616), calls=%async_computation | async-start | bytes 786432 | tf_op jit(solution)/shard_map/while/body/eval_jaxpr/all_to_all | solution.py:148
  24.8 10.5 %collective-permute-start = (f32[4,6144]{1,0:T(4,128)S(1)}, f32[4,6144]{1,0:T(4,128)S(1)}, u32[]{:S(2)}, u32[]{:S(2)}) collective-permute-start(f32[4,6144]{1,0:T(4,128)S(1)} %bitcast.481), channel_id=1, source_target_pairs={{4,0},{8,4},{12,8},{16,12},{20,16},{24,20},{28,24},{32,28},{36,32}... | collective-permute-start | bytes 294920 | tf_op jit(solution)/shard_map/while/body/eval_jaxpr/ppermute | solution.py:153
  33.3 3.5 %collective-permute-start.1 = (f32[4,6144]{1,0:T(4,128)S(1)}, f32[4,6144]{1,0:T(4,128)S(1)}, u32[]{:S(2)}, u32[]{:S(2)}) collective-permute-start(f32[4,6144]{1,0:T(4,128)S(1)} %get-tuple-element.781), channel_id=1, source_target_pairs={{0,4},{4,8},{8,12},{12,16},{16,20},{20,24},{24,28},{28,32},{32,36}... | collective-permute-start | bytes 294920 | tf_op jit(solution)/shard_map/while/body/eval_jaxpr/ppermute | solution.py:152
  41.4 1.0 copy-start.5
  50.9 11.8 %all-to-all-start = ((f32[3,4,6144]{2,0,1:T(4,128)}), f32[3,4,6144]{2,0,1:T(4,128)S(1)}, u32[]{:S(2)}, u32[]{:S(2)}) async-start(f32[3,4,6144]{2,0,1:T(4,128)} %copy.616), calls=%async_computation | async-start | bytes 786432 | tf_op jit(solution)/shard_map/while/body/eval_jaxpr/all_to_all | solution.py:148
  63.1 5.9 %collective-permute-start = (f32[4,6144]{1,0:T(4,128)S(1)}, f32[4,6144]{1,0:T(4,128)S(1)}, u32[]{:S(2)}, u32[]{:S(2)}) collective-permute-start(f32[4,6144]{1,0:T(4,128)S(1)} %bitcast.481), channel_id=1, source_target_pairs={{4,0},{8,4},{12,8},{16,12},{20,16},{24,20},{28,24},{32,28},{36,32}... | collective-permute-start | bytes 294920 | tf_op jit(solution)/shard_map/while/body/eval_jaxpr/ppermute | solution.py:153
  65.7 4.6 %collective-permute-start.1 = (f32[4,6144]{1,0:T(4,128)S(1)}, f32[4,6144]{1,0:T(4,128)S(1)}, u32[]{:S(2)}, u32[]{:S(2)}) collective-permute-start(f32[4,6144]{1,0:T(4,128)S(1)} %get-tuple-element.781), channel_id=1, source_target_pairs={{0,4},{4,8},{8,12},{12,16},{16,20},{20,24},{24,28},{28,32},{32,36}... | collective-permute-start | bytes 294920 | tf_op jit(solution)/shard_map/while/body/eval_jaxpr/ppermute | solution.py:152
  84.3 11.0 %all-to-all-start = ((f32[3,4,6144]{2,0,1:T(4,128)}), f32[3,4,6144]{2,0,1:T(4,128)S(1)}, u32[]{:S(2)}, u32[]{:S(2)}) async-start(f32[3,4,6144]{2,0,1:T(4,128)} %copy.616), calls=%async_computation | async-start | bytes 786432 | tf_op jit(solution)/shard_map/while/body/eval_jaxpr/all_to_all | solution.py:148
  95.6 6.5 %collective-permute-start = (f32[4,6144]{1,0:T(4,128)S(1)}, f32[4,6144]{1,0:T(4,128)S(1)}, u32[]{:S(2)}, u32[]{:S(2)}) collective-permute-start(f32[4,6144]{1,0:T(4,128)S(1)} %bitcast.481), channel_id=1, source_target_pairs={{4,0},{8,4},{12,8},{16,12},{20,16},{24,20},{28,24},{32,28},{36,32}... | collective-permute-start | bytes 294920 | tf_op jit(solution)/shard_map/while/body/eval_jaxpr/ppermute | solution.py:153
  97.6 5.8 %collective-permute-start.1 = (f32[4,6144]{1,0:T(4,128)S(1)}, f32[4,6144]{1,0:T(4,128)S(1)}, u32[]{:S(2)}, u32[]{:S(2)}) collective-permute-start(f32[4,6144]{1,0:T(4,128)S(1)} %get-tuple-element.781), channel_id=1, source_target_pairs={{0,4},{4,8},{8,12},{12,16},{16,20},{20,24},{24,28},{28,32},{32,36}... | collective-permute-start | bytes 294920 | tf_op jit(solution)/shard_map/while/body/eval_jaxpr/ppermute | solution.py:152
  113.4 8.2 %copy-start.13 = (f32[8,8,8]{2,1,0:T(8,128)S(1)}, f32[8,8,8]{2,1,0:T(8,128)}, u32[]{:S(2)}) copy-start(f32[8,8,8]{2,1,0:T(8,128)} %get-tuple-element.648) | copy-start | bytes 6148
  115.0 8.5 %copy-start.38 = (s32[1,128]{1,0:T(1,128)S(1)}, s32[1,128]{1,0:T(1,128)}, u32[]{:S(2)}) copy-start(s32[1,128]{1,0:T(1,128)} %param.20) | copy-start | bytes 1540
  116.0 11.8 %all-to-all-start.1 = ((f32[3,4,3072]{2,0,1:T(4,128)}), f32[3,4,3072]{2,0,1:T(4,128)}, u32[]{:S(2)}, u32[]{:S(2)}) async-start(f32[3,4,3072]{2,0,1:T(4,128)} %copy.398), calls=%async_computation.1 | async-start | bytes 393216 | tf_op jit(solution)/shard_map/all_to_all | solution.py:148
  120.8 2.8 %copy-start.8 = (f32[512,128]{1,0:T(8,128)S(1)}, f32[512,128]{1,0:T(8,128)}, u32[]{:S(2)}) copy-start(f32[512,128]{1,0:T(8,128)} %get-tuple-element.875) | copy-start | bytes 786436
  121.1 3.8 %copy-start.6 = (f32[3,512,128]{2,1,0:T(8,128)S(1)}, f32[3,512,128]{2,1,0:T(8,128)}, u32[]{:S(2)}) copy-start(f32[3,512,128]{2,1,0:T(8,128)} %get-tuple-element.878) | copy-start | bytes 2359300
  121.1 5.2 %copy-start.23 = (f32[8,8]{0,1:T(8,128)S(1)}, f32[8,8]{0,1:T(8,128)}, u32[]{:S(2)}) copy-start(f32[8,8]{0,1:T(8,128)} %copy-done.22) | copy-start | bytes 772
  129.7 7.1 %collective-permute-start.3 = (f32[4,3072]{1,0:T(4,128)S(1)}, f32[4,3072]{1,0:T(4,128)S(1)}, u32[]{:S(2)}, u32[]{:S(2)}) collective-permute-start(f32[4,3072]{1,0:T(4,128)S(1)} %bitcast.492), channel_id=1, source_target_pairs={{4,0},{8,4},{12,8},{16,12},{20,16},{24,20},{28,24},{32,28},{36,32}... | collective-permute-start | bytes 147464 | tf_op jit(solution)/shard_map/ppermute | solution.py:153
  131.7 5.5 %collective-permute-start.2 = (f32[4,3072]{1,0:T(4,128)S(1)}, f32[4,3072]{1,0:T(4,128)S(1)}, u32[]{:S(2)}, u32[]{:S(2)}) collective-permute-start(f32[4,3072]{1,0:T(4,128)S(1)} %get-tuple-element.641), channel_id=1, source_target_pairs={{0,4},{4,8},{8,12},{12,16},{16,20},{20,24},{24,28},{28,32},{32,36}... | collective-permute-start | bytes 147464 | tf_op jit(solution)/shard_map/ppermute | solution.py:152
  147.0 8.7 %all-to-all-start.2 = ((f32[4,1,642]{2,1,0:T(1,128)}), f32[4,1,642]{2,1,0:T(1,128)S(1)}, u32[]{:S(2)}, u32[]{:S(2)}) async-start(f32[4,1,642]{2,1,0:T(1,128)} %broadcast_in_dim.301), calls=%async_computation.2 | async-start | bytes 24576 | tf_op jit(solution)/shard_map/all_to_all | solution.py:248
  157.7 39.2 %all-to-all-start.3 = ((f32[128,1,2]{2,1,0:T(1,128)}), f32[128,1,2]{2,1,0:T(1,128)S(1)}, u32[]{:S(2)}, u32[]{:S(2)}) async-start(f32[128,1,2]{2,1,0:T(1,128)} %broadcast_in_dim.302), calls=%async_computation.3 | async-start | bytes 131072 | tf_op jit(solution)/shard_map/all_to_all | solution.py:251
  199.4 2.3 %copy-start.9 = (f32[3,512,128]{2,1,0:T(8,128)S(1)}, f32[3,512,128]{2,1,0:T(8,128)}, u32[]{:S(2)}) copy-start(f32[3,512,128]{2,1,0:T(8,128)} %get-tuple-element.877) | copy-start | bytes 2359300
  (42 other events, 30.1 us)

commit v3 on v2

--- a/solution.py
+++ b/solution.py
@@ -146,7 +146,8 @@
     picked = local[:, send_list[0]]
     outgoing = picked.T.reshape(3, lax.axis_size("narrow"), -1)
     swapped = lax.all_to_all(outgoing, "narrow", split_axis=1, concat_axis=1, tiled=True)
-    swapped, cover = lax.optimization_barrier((swapped, cover))
+    if fields > 1:
+        swapped, cover = lax.optimization_barrier((swapped, cover))
     up = [(i, i + 1) for i in range(wide - 1)]
     down = [(i + 1, i) for i in range(wide - 1)]
     before = lax.ppermute(swapped[2], "wide", up)

time: 204 us -> 202 us (level)
    unnamed x83 -> x103, local copies, waits for them, and re-layouts: 11.2 us -> 10.9 us
  transfers between devices with their start and end apart: 14 -> 14, of which waited for: 11 -> 10; matrix products, arithmetic and copies ran while one was open for 10% -> 9% of each run, Pallas kernels for 0% -> 0%
where the time goes in v3:
time: 202 us; the launch traced here: 201 us
  starting transfers between devices  71.9 us (36%)
  local copies, waits for them, and re-layouts  57.8 us (29%)
  waiting for transfers between devices  30 us (15%)
  matrix products  19.3 us (10%)
  other arithmetic  17.2 us (9%)
  between operations  3.13 us (2%)
    all_to_all x1, starting transfers between devices, body(): norms = jnp.sum(lax.all_to_all(spread, 'wide', 0, 0, tiled=True), axis=0)  23.9 us
    all_to_all x4, starting transfers between devices, neighbour_traces(): lax.all_to_all(outgoing, 'narrow', split_axis=1, concat_axis=1, tiled=True)  15.3 us
    ppermute x4, starting transfers between devices, neighbour_traces(): after = lax.ppermute(swapped[0], 'wide', down)  14.9 us
    all_to_all x1, waiting for transfers between devices, body(): norms = jnp.sum(lax.all_to_all(spread, 'wide', 0, 0, tiled=True), axis=0)  14.5 us
    while x87, local copies, waits for them, and re-layouts  13.9 us
    ppermute x4, starting transfers between devices, neighbour_traces(): before = lax.ppermute(swapped[2], 'wide', up)  13.4 us
    unnamed x103, local copies, waits for them, and re-layouts  10.9 us
    gather x7, local copies, waits for them, and re-layouts, neighbour_traces(): gathered = pool[:, columns]  6.78 us
  transfers between devices with their start and end apart: 14, of which 10 were waited for; matrix products, arithmetic and copies ran while one was open for 9% of the time, Pallas kernels for 0%

profile of v3, /device:TPU:1, one launch (start us, length us, event | category | flops | bytes accessed | tf_op | source)
XLA Modules:
  0.0 200.9 jit_solution(2581472927817470607)
XLA Ops:
  8.5 104.4 %while.27 = (s32[]{:T(128)}, f32[512,128]{1,0:T(8,128)S(1)}, f32[512,128]{1,0:T(8,128)}, f32[512,128]{1,0:T(8,128)S(1)}, f32[3,512,128]{2,1,0:T(8,128)}, /*index...) while((s32[]{:T(128)}, f32[512,128]{1,0:T(8,128)S(1)}, ...), condition=%wide.region_1.2_spmd.clone.clone.clone, body=%wide.region_0.1_spmd.sunk.clone.clone.clone.sunk | while | flops 79930784 | bytes 40470192 | solution.py:233
  10.8 1.6 gather_fusion
  13.4 4.8 %all-to-all-start = ((f32[3,4,6144]{2,0,1:T(4,128)}), f32[3,4,6144]{2,0,1:T(4,128)S(1)}, u32[]{:S(2)}, u32[]{:S(2)}) async-start(f32[3,4,6144]{2,0,1:T(4,128)} %copy.622), calls=%async_computation | async-start | bytes 786432 | tf_op jit(solution)/shard_map/while/body/eval_jaxpr/all_to_all | solution.py:148
  24.8 8.5 %collective-permute-start = (f32[4,6144]{1,0:T(4,128)S(1)}, f32[4,6144]{1,0:T(4,128)S(1)}, u32[]{:S(2)}, u32[]{:S(2)}) collective-permute-start(f32[4,6144]{1,0:T(4,128)S(1)} %bitcast.494), channel_id=1, source_target_pairs={{4,0},{8,4},{12,8},{16,12},{20,16},{24,20},{28,24},{32,28},{36,32}... | collective-permute-start | bytes 294920 | tf_op jit(solution)/shard_map/while/body/eval_jaxpr/ppermute | solution.py:154
  33.4 1.9 collective-permute-start.1
  35.4 1.6 collective-permute-done.1
  48.4 1.6 gather_fusion
  51.1 3.5 %all-to-all-start = ((f32[3,4,6144]{2,0,1:T(4,128)}), f32[3,4,6144]{2,0,1:T(4,128)S(1)}, u32[]{:S(2)}, u32[]{:S(2)}) async-start(f32[3,4,6144]{2,0,1:T(4,128)} %copy.622), calls=%async_computation | async-start | bytes 786432 | tf_op jit(solution)/shard_map/while/body/eval_jaxpr/all_to_all | solution.py:148
  59.7 3.2 %all-to-all-done = f32[3,4,6144]{2,0,1:T(4,128)S(1)} async-done(((f32[3,4,6144]{2,0,1:T(4,128)}), f32[3,4,6144]{2,0,1:T(4,128)S(1)}, u32[]{:S(2)}, u32[]{:S(2)}) %all-to-all-start) | async-done | bytes 294944 | tf_op jit(solution)/shard_map/while/body/eval_jaxpr/all_to_all | solution.py:148
  63.2 2.6 %collective-permute-start = (f32[4,6144]{1,0:T(4,128)S(1)}, f32[4,6144]{1,0:T(4,128)S(1)}, u32[]{:S(2)}, u32[]{:S(2)}) collective-permute-start(f32[4,6144]{1,0:T(4,128)S(1)} %bitcast.494), channel_id=1, source_target_pairs={{4,0},{8,4},{12,8},{16,12},{20,16},{24,20},{28,24},{32,28},{36,32}... | collective-permute-start | bytes 294920 | tf_op jit(solution)/shard_map/while/body/eval_jaxpr/ppermute | solution.py:154
  65.8 3.0 %collective-permute-start.1 = (f32[4,6144]{1,0:T(4,128)S(1)}, f32[4,6144]{1,0:T(4,128)S(1)}, u32[]{:S(2)}, u32[]{:S(2)}) collective-permute-start(f32[4,6144]{1,0:T(4,128)S(1)} %get-tuple-element.778), channel_id=1, source_target_pairs={{0,4},{4,8},{8,12},{12,16},{16,20},{20,24},{24,28},{28,32},{32,36}... | collective-permute-start | bytes 294920 | tf_op jit(solution)/shard_map/while/body/eval_jaxpr/ppermute | solution.py:153
  81.9 1.6 gather_fusion
  84.6 3.5 %all-to-all-start = ((f32[3,4,6144]{2,0,1:T(4,128)}), f32[3,4,6144]{2,0,1:T(4,128)S(1)}, u32[]{:S(2)}, u32[]{:S(2)}) async-start(f32[3,4,6144]{2,0,1:T(4,128)} %copy.622), calls=%async_computation | async-start | bytes 786432 | tf_op jit(solution)/shard_map/while/body/eval_jaxpr/all_to_all | solution.py:148
  93.2 2.3 %all-to-all-done = f32[3,4,6144]{2,0,1:T(4,128)S(1)} async-done(((f32[3,4,6144]{2,0,1:T(4,128)}), f32[3,4,6144]{2,0,1:T(4,128)S(1)}, u32[]{:S(2)}, u32[]{:S(2)}) %all-to-all-start) | async-done | bytes 294944 | tf_op jit(solution)/shard_map/while/body/eval_jaxpr/all_to_all | solution.py:148
  95.9 1.9 collective-permute-start
  97.8 4.2 %collective-permute-start.1 = (f32[4,6144]{1,0:T(4,128)S(1)}, f32[4,6144]{1,0:T(4,128)S(1)}, u32[]{:S(2)}, u32[]{:S(2)}) collective-permute-start(f32[4,6144]{1,0:T(4,128)S(1)} %get-tuple-element.778), channel_id=1, source_target_pairs={{0,4},{4,8},{8,12},{12,16},{16,20},{20,24},{24,28},{28,32},{32,36}... | collective-permute-start | bytes 294920 | tf_op jit(solution)/shard_map/while/body/eval_jaxpr/ppermute | solution.py:153
  113.7 1.6 gather_fusion.3
  116.3 3.5 %all-to-all-start.1 = ((f32[3,4,3072]{2,0,1:T(4,128)}), f32[3,4,3072]{2,0,1:T(4,128)S(1)}, u32[]{:S(2)}, u32[]{:S(2)}) async-start(f32[3,4,3072]{2,0,1:T(4,128)} %copy.405), calls=%async_computation.1 | async-start | bytes 393216 | tf_op jit(solution)/shard_map/all_to_all | solution.py:148
  126.7 1.9 collective-permute-start.3
  128.7 4.3 %collective-permute-start.2 = (f32[4,3072]{1,0:T(4,128)S(1)}, f32[4,3072]{1,0:T(4,128)S(1)}, u32[]{:S(2)}, u32[]{:S(2)}) collective-permute-start(f32[4,3072]{1,0:T(4,128)S(1)} %bitcast.506), channel_id=1, source_target_pairs={{0,4},{4,8},{8,12},{12,16},{16,20},{20,24},{24,28},{28,32},{32,36}... | collective-permute-start | bytes 147464 | tf_op jit(solution)/shard_map/ppermute | solution.py:153
  145.8 4.5 %all-to-all-start.2 = ((f32[4,1,642]{2,1,0:T(1,128)}), f32[4,1,642]{2,1,0:T(1,128)S(1)}, u32[]{:S(2)}, u32[]{:S(2)}) async-start(f32[4,1,642]{2,1,0:T(1,128)} %broadcast_in_dim.301), calls=%async_computation.2 | async-start | bytes 24576 | tf_op jit(solution)/shard_map/all_to_all | solution.py:249
  150.4 4.1 %all-to-all-done.2 = f32[4,1,642]{2,1,0:T(1,128)S(1)} async-done(((f32[4,1,642]{2,1,0:T(1,128)}), f32[4,1,642]{2,1,0:T(1,128)S(1)}, u32[]{:S(2)}, u32[]{:S(2)}) %all-to-all-start.2) | async-done | bytes 10304 | tf_op jit(solution)/shard_map/all_to_all | solution.py:249
  156.4 23.9 %all-to-all-start.3 = ((f32[128,1,2]{2,1,0:T(1,128)}), f32[128,1,2]{2,1,0:T(1,128)S(1)}, u32[]{:S(2)}, u32[]{:S(2)}) async-start(f32[128,1,2]{2,1,0:T(1,128)} %broadcast_in_dim.302), calls=%async_computation.3 | async-start | bytes 131072 | tf_op jit(solution)/shard_map/all_to_all | solution.py:252
  180.8 14.5 %all-to-all-done.3 = f32[128,1,2]{2,1,0:T(1,128)S(1)} async-done(((f32[128,1,2]{2,1,0:T(1,128)}), f32[128,1,2]{2,1,0:T(1,128)S(1)}, u32[]{:S(2)}, u32[]{:S(2)}) %all-to-all-start.3) | async-done | bytes 1056 | tf_op jit(solution)/shard_map/all_to_all | solution.py:252
  (450 shorter events, 92.1 us)
Async XLA Ops:
  0.6 198.0 %copy-start = (f32[1,128,128]{2,1,0:T(8,128)S(1)}, f32[1,128,128]{2,1,0:T(8,128)}, u32[]{:S(2)}) copy-start(f32[1,128,128]{2,1,0:T(8,128)} %param.21) | copy-start | bytes 196612
  2.3 2.8 %copy-start.34 = (f32[8]{0:T(128)}, f32[8]{0:T(128)S(1)}, u32[]{:S(2)}) copy-start(f32[8]{0:T(128)S(1)} %get-tuple-element.659) | copy-start | bytes 100
  2.4 2.8 %copy-start.36 = (f32[8]{0:T(128)}, f32[8]{0:T(128)S(1)}, u32[]{:S(2)}) copy-start(f32[8]{0:T(128)S(1)} %get-tuple-element.660) | copy-start | bytes 100
  13.4 11.1 %all-to-all-start = ((f32[3,4,6144]{2,0,1:T(4,128)}), f32[3,4,6144]{2,0,1:T(4,128)S(1)}, u32[]{:S(2)}, u32[]{:S(2)}) async-start(f32[3,4,6144]{2,0,1:T(4,128)} %copy.622), calls=%async_computation | async-start | bytes 786432 | tf_op jit(solution)/shard_map/while/body/eval_jaxpr/all_to_all | solution.py:148
  24.8 10.5 %collective-permute-start = (f32[4,6144]{1,0:T(4,128)S(1)}, f32[4,6144]{1,0:T(4,128)S(1)}, u32[]{:S(2)}, u32[]{:S(2)}) collective-permute-start(f32[4,6144]{1,0:T(4,128)S(1)} %bitcast.494), channel_id=1, source_target_pairs={{4,0},{8,4},{12,8},{16,12},{20,16},{24,20},{28,24},{32,28},{36,32}... | collective-permute-start | bytes 294920 | tf_op jit(solution)/shard_map/while/body/eval_jaxpr/ppermute | solution.py:154
  33.4 3.5 %collective-permute-start.1 = (f32[4,6144]{1,0:T(4,128)S(1)}, f32[4,6144]{1,0:T(4,128)S(1)}, u32[]{:S(2)}, u32[]{:S(2)}) collective-permute-start(f32[4,6144]{1,0:T(4,128)S(1)} %get-tuple-element.778), channel_id=1, source_target_pairs={{0,4},{4,8},{8,12},{12,16},{16,20},{20,24},{24,28},{28,32},{32,36}... | collective-permute-start | bytes 294920 | tf_op jit(solution)/shard_map/while/body/eval_jaxpr/ppermute | solution.py:153
  41.5 1.0 copy-start.5
  51.1 11.8 %all-to-all-start = ((f32[3,4,6144]{2,0,1:T(4,128)}), f32[3,4,6144]{2,0,1:T(4,128)S(1)}, u32[]{:S(2)}, u32[]{:S(2)}) async-start(f32[3,4,6144]{2,0,1:T(4,128)} %copy.622), calls=%async_computation | async-start | bytes 786432 | tf_op jit(solution)/shard_map/while/body/eval_jaxpr/all_to_all | solution.py:148
  63.2 5.9 %collective-permute-start = (f32[4,6144]{1,0:T(4,128)S(1)}, f32[4,6144]{1,0:T(4,128)S(1)}, u32[]{:S(2)}, u32[]{:S(2)}) collective-permute-start(f32[4,6144]{1,0:T(4,128)S(1)} %bitcast.494), channel_id=1, source_target_pairs={{4,0},{8,4},{12,8},{16,12},{20,16},{24,20},{28,24},{32,28},{36,32}... | collective-permute-start | bytes 294920 | tf_op jit(solution)/shard_map/while/body/eval_jaxpr/ppermute | solution.py:154
  65.8 4.6 %collective-permute-start.1 = (f32[4,6144]{1,0:T(4,128)S(1)}, f32[4,6144]{1,0:T(4,128)S(1)}, u32[]{:S(2)}, u32[]{:S(2)}) collective-permute-start(f32[4,6144]{1,0:T(4,128)S(1)} %get-tuple-element.778), channel_id=1, source_target_pairs={{0,4},{4,8},{8,12},{12,16},{16,20},{20,24},{24,28},{28,32},{32,36}... | collective-permute-start | bytes 294920 | tf_op jit(solution)/shard_map/while/body/eval_jaxpr/ppermute | solution.py:153
  75.0 1.0 copy-start.5
  84.6 11.0 %all-to-all-start = ((f32[3,4,6144]{2,0,1:T(4,128)}), f32[3,4,6144]{2,0,1:T(4,128)S(1)}, u32[]{:S(2)}, u32[]{:S(2)}) async-start(f32[3,4,6144]{2,0,1:T(4,128)} %copy.622), calls=%async_computation | async-start | bytes 786432 | tf_op jit(solution)/shard_map/while/body/eval_jaxpr/all_to_all | solution.py:148
  95.9 6.5 %collective-permute-start = (f32[4,6144]{1,0:T(4,128)S(1)}, f32[4,6144]{1,0:T(4,128)S(1)}, u32[]{:S(2)}, u32[]{:S(2)}) collective-permute-start(f32[4,6144]{1,0:T(4,128)S(1)} %bitcast.494), channel_id=1, source_target_pairs={{4,0},{8,4},{12,8},{16,12},{20,16},{24,20},{28,24},{32,28},{36,32}... | collective-permute-start | bytes 294920 | tf_op jit(solution)/shard_map/while/body/eval_jaxpr/ppermute | solution.py:154
  97.8 5.8 %collective-permute-start.1 = (f32[4,6144]{1,0:T(4,128)S(1)}, f32[4,6144]{1,0:T(4,128)S(1)}, u32[]{:S(2)}, u32[]{:S(2)}) collective-permute-start(f32[4,6144]{1,0:T(4,128)S(1)} %get-tuple-element.778), channel_id=1, source_target_pairs={{0,4},{4,8},{8,12},{12,16},{16,20},{20,24},{24,28},{28,32},{32,36}... | collective-permute-start | bytes 294920 | tf_op jit(solution)/shard_map/while/body/eval_jaxpr/ppermute | solution.py:153
  113.7 9.4 %copy-start.13 = (f32[8,8,8]{2,1,0:T(8,128)S(1)}, f32[8,8,8]{2,1,0:T(8,128)}, u32[]{:S(2)}) copy-start(f32[8,8,8]{2,1,0:T(8,128)} %get-tuple-element.643) | copy-start | bytes 6148
  116.3 9.8 %all-to-all-start.1 = ((f32[3,4,3072]{2,0,1:T(4,128)}), f32[3,4,3072]{2,0,1:T(4,128)S(1)}, u32[]{:S(2)}, u32[]{:S(2)}) async-start(f32[3,4,3072]{2,0,1:T(4,128)} %copy.405), calls=%async_computation.1 | async-start | bytes 393216 | tf_op jit(solution)/shard_map/all_to_all | solution.py:148
  121.1 4.3 %copy-start.6 = (f32[3,512,128]{2,1,0:T(8,128)S(1)}, f32[3,512,128]{2,1,0:T(8,128)}, u32[]{:S(2)}) copy-start(f32[3,512,128]{2,1,0:T(8,128)} %get-tuple-element.875) | copy-start | bytes 2359300
  122.1 1.9 copy-start.8
  126.7 7.7 %collective-permute-start.3 = (f32[4,3072]{1,0:T(4,128)S(1)}, f32[4,3072]{1,0:T(4,128)S(1)}, u32[]{:S(2)}, u32[]{:S(2)}) collective-permute-start(f32[4,3072]{1,0:T(4,128)S(1)} %bitcast.505), channel_id=1, source_target_pairs={{4,0},{8,4},{12,8},{16,12},{20,16},{24,20},{28,24},{32,28},{36,32}... | collective-permute-start | bytes 147464 | tf_op jit(solution)/shard_map/ppermute | solution.py:154
  128.7 5.8 %collective-permute-start.2 = (f32[4,3072]{1,0:T(4,128)S(1)}, f32[4,3072]{1,0:T(4,128)S(1)}, u32[]{:S(2)}, u32[]{:S(2)}) collective-permute-start(f32[4,3072]{1,0:T(4,128)S(1)} %bitcast.506), channel_id=1, source_target_pairs={{0,4},{4,8},{8,12},{12,16},{16,20},{20,24},{24,28},{28,32},{32,36}... | collective-permute-start | bytes 147464 | tf_op jit(solution)/shard_map/ppermute | solution.py:153
  139.5 1.0 copy-start.18
  145.8 8.7 %all-to-all-start.2 = ((f32[4,1,642]{2,1,0:T(1,128)}), f32[4,1,642]{2,1,0:T(1,128)S(1)}, u32[]{:S(2)}, u32[]{:S(2)}) async-start(f32[4,1,642]{2,1,0:T(1,128)} %broadcast_in_dim.301), calls=%async_computation.2 | async-start | bytes 24576 | tf_op jit(solution)/shard_map/all_to_all | solution.py:249
  156.4 38.8 %all-to-all-start.3 = ((f32[128,1,2]{2,1,0:T(1,128)}), f32[128,1,2]{2,1,0:T(1,128)S(1)}, u32[]{:S(2)}, u32[]{:S(2)}) async-start(f32[128,1,2]{2,1,0:T(1,128)} %broadcast_in_dim.302), calls=%async_computation.3 | async-start | bytes 131072 | tf_op jit(solution)/shard_map/all_to_all | solution.py:252
  197.8 2.3 %copy-start.9 = (f32[3,512,128]{2,1,0:T(8,128)S(1)}, f32[3,512,128]{2,1,0:T(8,128)}, u32[]{:S(2)}) copy-start(f32[3,512,128]{2,1,0:T(8,128)} %get-tuple-element.874) | copy-start | bytes 2359300
  (51 other events, 38.7 us)

commit v4 on v1

--- a/solution.py
+++ b/solution.py
@@ -86,16 +86,21 @@
     return cube
 
 
-def orient_faces(neighbour, orientation, subface, half_low, half_high):
+def orient_masks(orientation, subface):
     bit_one = (orientation % 2)[:, None, None, :] == 1
     bit_two = (orientation // 2 % 2)[:, None, None, :] == 1
     bit_four = (orientation // 4)[:, None, None, :] == 1
+    hanging = (subface > 0)[:, None, None, :]
+    quad_first = ((subface - 1) % 2)[:, None, None, :] == 0
+    quad_second = ((subface - 1) // 2)[:, None, None, :] == 0
+    return bit_one, bit_two, bit_four, hanging, quad_first, quad_second
+
+
+def orient_faces(neighbour, masks, half_low, half_high):
+    bit_one, bit_two, bit_four, hanging, quad_first, quad_second = masks
     turned = jnp.where(bit_one, neighbour[:, ::-1], neighbour)
     turned = jnp.where(bit_two, turned[:, :, ::-1], turned)
     turned = jnp.where(bit_four, jnp.swapaxes(turned, 1, 2), turned)
-    hanging = (subface > 0)[:, None, None, :]
-    quad_first = ((subface - 1) % 2)[:, None, None, :] == 0
-    quad_second = ((subface - 1) // 2)[:, None, None, :] == 0
     low_first = jnp.einsum("ai,fibe->fabe", half_low, turned, precision=HIGHEST)
     high_first = jnp.einsum("ai,fibe->fabe", half_high, turned, precision=HIGHEST)
     first_pass = jnp.where(quad_first, low_first, high_first)
@@ -193,6 +198,11 @@
     inv_diag = 1.0 / (diag_pattern(tables)[:, None] * scale[None, :])
     face_mass = weights[:, None] * weights[None, :]
 
+    masks = {
+        number: orient_masks(jnp.tile(orientation, (1, number)), jnp.tile(subface, (1, number)))
+        for number in (1, 2)
+    }
+
     def operator(fields):
         number = len(fields)
         field = jnp.concatenate(fields, axis=1) if number > 1 else fields[0]
@@ -201,8 +211,7 @@
         traces = face_traces(cube)
         neighbour = orient_faces(
             neighbour_traces(traces, face_source, send_list, number),
-            jnp.tile(orientation, (1, number)),
-            jnp.tile(subface, (1, number)),
+            masks[number],
             half_low,
             half_high,
         )

time: 198 us -> 201 us (1.015)
  local copies, waits for them, and re-layouts: 47.3 us -> 58.4 us
  waiting for transfers between devices: 39 us -> 29.7 us
    all_to_all x4, waiting for transfers between devices: 12.8 us -> 4.08 us  [neighbour_traces(): lax.all_to_all(outgoing, 'narrow', split_axis=1, concat_axis=1, tiled=True)]
    while x69 -> x57, local copies, waits for them, and re-layouts: 6.94 us -> 13.9 us
    unnamed x79 -> x81, local copies, waits for them, and re-layouts: 6.52 us -> 8.51 us
  transfers between devices with their start and end apart: 14 -> 14, of which waited for: 12 -> 12; matrix products, arithmetic and copies ran while one was open for 6% -> 12% of each run, Pallas kernels for 0% -> 0%
where the time goes in v4:
time: 201 us; the launch traced here: 200 us
  starting transfers between devices  69.8 us (35%)
  local copies, waits for them, and re-layouts  58.4 us (29%)
  waiting for transfers between devices  29.7 us (15%)
  matrix products  20 us (10%)
  other arithmetic  17.3 us (9%)
  between operations  3.07 us (2%)
    all_to_all x1, starting transfers between devices, body(): norms = jnp.sum(lax.all_to_all(spread, 'wide', 0, 0, tiled=True), axis=0)  21.7 us
    all_to_all x4, starting transfers between devices, neighbour_traces(): lax.all_to_all(outgoing, 'narrow', split_axis=1, concat_axis=1, tiled=True)  15.3 us
    ppermute x4, starting transfers between devices, neighbour_traces(): after = lax.ppermute(swapped[0], 'wide', down)  15 us
    ppermute x4, starting transfers between devices, neighbour_traces(): before = lax.ppermute(swapped[2], 'wide', up)  14.6 us
    all_to_all x1, waiting for transfers between devices, body(): norms = jnp.sum(lax.all_to_all(spread, 'wide', 0, 0, tiled=True), axis=0)  14.3 us
    while x57, local copies, waits for them, and re-layouts  13.9 us
    unnamed x81, local copies, waits for them, and re-layouts  8.51 us
    gather x7, local copies, waits for them, and re-layouts, neighbour_traces(): gathered = pool[:, columns]  6.78 us
  transfers between devices with their start and end apart: 14, of which 12 were waited for; matrix products, arithmetic and copies ran while one was open for 12% of the time, Pallas kernels for 0%

profile of v4, /device:TPU:1, one launch (start us, length us, event | category | flops | bytes accessed | tf_op | source)
XLA Modules:
  0.0 199.7 jit_solution(5932307945103918092)
XLA Ops:
  7.6 107.5 %while.24 = (s32[]{:T(128)}, f32[512,128]{1,0:T(8,128)S(1)}, f32[512,128]{1,0:T(8,128)}, f32[512,128]{1,0:T(8,128)S(1)}, f32[3,512,128]{2,1,0:T(8,128)}, /*index...) while((s32[]{:T(128)}, f32[512,128]{1,0:T(8,128)S(1)}, ...), condition=%wide.region_1.2_spmd.clone.clone.clone, body=%wide.region_0.1_spmd.sunk.clone.clone.clone.sunk | while | flops 79929248 | bytes 37651236 | solution.py:237
  9.3 1.6 gather_fusion
  12.0 4.8 %all-to-all-start = ((f32[3,4,6144]{2,0,1:T(4,128)}), f32[3,4,6144]{2,0,1:T(4,128)S(1)}, u32[]{:S(2)}, u32[]{:S(2)}) async-start(f32[3,4,6144]{2,0,1:T(4,128)} %copy.566), calls=%async_computation | async-start | bytes 786432 | tf_op jit(solution)/shard_map/while/body/eval_jaxpr/all_to_all | solution.py:153
  23.4 8.5 %collective-permute-start = (f32[4,6144]{1,0:T(4,128)S(1)}, f32[4,6144]{1,0:T(4,128)S(1)}, u32[]{:S(2)}, u32[]{:S(2)}) collective-permute-start(f32[4,6144]{1,0:T(4,128)S(1)} %bitcast.453), channel_id=1, source_target_pairs={{4,0},{8,4},{12,8},{16,12},{20,16},{24,20},{28,24},{32,28},{36,32}... | collective-permute-start | bytes 294920 | tf_op jit(solution)/shard_map/while/body/eval_jaxpr/ppermute | solution.py:157
  31.9 1.9 collective-permute-start.1
  43.5 1.7 fusion.216
  48.0 1.6 gather_fusion
  50.8 3.5 %all-to-all-start = ((f32[3,4,6144]{2,0,1:T(4,128)}), f32[3,4,6144]{2,0,1:T(4,128)S(1)}, u32[]{:S(2)}, u32[]{:S(2)}) async-start(f32[3,4,6144]{2,0,1:T(4,128)} %copy.566), calls=%async_computation | async-start | bytes 786432 | tf_op jit(solution)/shard_map/while/body/eval_jaxpr/all_to_all | solution.py:153
  60.4 2.2 %all-to-all-done = f32[3,4,6144]{2,0,1:T(4,128)S(1)} async-done(((f32[3,4,6144]{2,0,1:T(4,128)}), f32[3,4,6144]{2,0,1:T(4,128)S(1)}, u32[]{:S(2)}, u32[]{:S(2)}) %all-to-all-start) | async-done | bytes 294944 | tf_op jit(solution)/shard_map/while/body/eval_jaxpr/all_to_all | solution.py:153
  62.8 2.6 %collective-permute-start = (f32[4,6144]{1,0:T(4,128)S(1)}, f32[4,6144]{1,0:T(4,128)S(1)}, u32[]{:S(2)}, u32[]{:S(2)}) collective-permute-start(f32[4,6144]{1,0:T(4,128)S(1)} %bitcast.453), channel_id=1, source_target_pairs={{4,0},{8,4},{12,8},{16,12},{20,16},{24,20},{28,24},{32,28},{36,32}... | collective-permute-start | bytes 294920 | tf_op jit(solution)/shard_map/while/body/eval_jaxpr/ppermute | solution.py:157
  65.4 3.0 %collective-permute-start.1 = (f32[4,6144]{1,0:T(4,128)S(1)}, f32[4,6144]{1,0:T(4,128)S(1)}, u32[]{:S(2)}, u32[]{:S(2)}) collective-permute-start(f32[4,6144]{1,0:T(4,128)S(1)} %bitcast.454), channel_id=1, source_target_pairs={{0,4},{4,8},{8,12},{12,16},{16,20},{20,24},{24,28},{28,32},{32,36}... | collective-permute-start | bytes 294920 | tf_op jit(solution)/shard_map/while/body/eval_jaxpr/ppermute | solution.py:156
  78.0 1.7 fusion.216
  85.3 3.5 %all-to-all-start = ((f32[3,4,6144]{2,0,1:T(4,128)}), f32[3,4,6144]{2,0,1:T(4,128)S(1)}, u32[]{:S(2)}, u32[]{:S(2)}) async-start(f32[3,4,6144]{2,0,1:T(4,128)} %copy.566), calls=%async_computation | async-start | bytes 786432 | tf_op jit(solution)/shard_map/while/body/eval_jaxpr/all_to_all | solution.py:153
  96.6 1.9 collective-permute-start
  98.5 4.1 %collective-permute-start.1 = (f32[4,6144]{1,0:T(4,128)S(1)}, f32[4,6144]{1,0:T(4,128)S(1)}, u32[]{:S(2)}, u32[]{:S(2)}) collective-permute-start(f32[4,6144]{1,0:T(4,128)S(1)} %bitcast.454), channel_id=1, source_target_pairs={{0,4},{4,8},{8,12},{12,16},{16,20},{20,24},{24,28},{28,32},{32,36}... | collective-permute-start | bytes 294920 | tf_op jit(solution)/shard_map/while/body/eval_jaxpr/ppermute | solution.py:156
  112.3 1.7 fusion.216
  118.1 3.5 %all-to-all-start.1 = ((f32[3,4,3072]{2,0,1:T(4,128)}), f32[3,4,3072]{2,0,1:T(4,128)S(1)}, u32[]{:S(2)}, u32[]{:S(2)}) async-start(f32[3,4,3072]{2,0,1:T(4,128)} %copy.405), calls=%async_computation.1 | async-start | bytes 393216 | tf_op jit(solution)/shard_map/all_to_all | solution.py:153
  126.8 5.6 %collective-permute-start.2 = (f32[4,3072]{1,0:T(4,128)S(1)}, f32[4,3072]{1,0:T(4,128)S(1)}, u32[]{:S(2)}, u32[]{:S(2)}) collective-permute-start(f32[4,3072]{1,0:T(4,128)S(1)} %bitcast.465), channel_id=1, source_target_pairs={{0,4},{4,8},{8,12},{12,16},{16,20},{20,24},{24,28},{28,32},{32,36}... | collective-permute-start | bytes 147464 | tf_op jit(solution)/shard_map/ppermute | solution.py:156
  132.4 1.9 collective-permute-start.3
  135.2 2.6 %collective-permute-done.3 = f32[4,3072]{1,0:T(4,128)S(1)} collective-permute-done((f32[4,3072]{1,0:T(4,128)S(1)}, f32[4,3072]{1,0:T(4,128)S(1)}, u32[]{:S(2)}, u32[]{:S(2)}) %collective-permute-start.3) | collective-permute-done | bytes 49184 | tf_op jit(solution)/shard_map/ppermute | solution.py:157
  149.2 3.3 %all-to-all-start.2 = ((f32[4,1,642]{2,1,0:T(1,128)}), f32[4,1,642]{2,1,0:T(1,128)S(1)}, u32[]{:S(2)}, u32[]{:S(2)}) async-start(f32[4,1,642]{2,1,0:T(1,128)} %broadcast_in_dim.263), calls=%async_computation.2 | async-start | bytes 24576 | tf_op jit(solution)/shard_map/all_to_all | solution.py:253
  152.5 4.1 %all-to-all-done.2 = f32[4,1,642]{2,1,0:T(1,128)S(1)} async-done(((f32[4,1,642]{2,1,0:T(1,128)}), f32[4,1,642]{2,1,0:T(1,128)S(1)}, u32[]{:S(2)}, u32[]{:S(2)}) %all-to-all-start.2) | async-done | bytes 10304 | tf_op jit(solution)/shard_map/all_to_all | solution.py:253
  157.4 21.7 %all-to-all-start.3 = ((f32[128,1,2]{2,1,0:T(1,128)}), f32[128,1,2]{2,1,0:T(1,128)S(1)}, u32[]{:S(2)}, u32[]{:S(2)}) async-start(f32[128,1,2]{2,1,0:T(1,128)} %broadcast_in_dim.264), calls=%async_computation.3 | async-start | bytes 131072 | tf_op jit(solution)/shard_map/all_to_all | solution.py:256
  179.8 14.3 %all-to-all-done.3 = f32[128,1,2]{2,1,0:T(1,128)S(1)} async-done(((f32[128,1,2]{2,1,0:T(1,128)}), f32[128,1,2]{2,1,0:T(1,128)S(1)}, u32[]{:S(2)}, u32[]{:S(2)}) %all-to-all-start.3) | async-done | bytes 1056 | tf_op jit(solution)/shard_map/all_to_all | solution.py:256
  (395 shorter events, 94.2 us)
Async XLA Ops:
  0.6 196.8 %copy-start = (f32[1,128,128]{2,1,0:T(8,128)S(1)}, f32[1,128,128]{2,1,0:T(8,128)}, u32[]{:S(2)}) copy-start(f32[1,128,128]{2,1,0:T(8,128)} %param.21) | copy-start | bytes 196612
  0.7 4.5 %copy-start.21 = (f32[8]{0:T(128)}, f32[8]{0:T(128)S(1)}, u32[]{:S(2)}) copy-start(f32[8]{0:T(128)S(1)} %get-tuple-element.583) | copy-start | bytes 100
  0.7 4.5 %copy-start.23 = (f32[8]{0:T(128)}, f32[8]{0:T(128)S(1)}, u32[]{:S(2)}) copy-start(f32[8]{0:T(128)S(1)} %get-tuple-element.584) | copy-start | bytes 100
  12.0 11.1 %all-to-all-start = ((f32[3,4,6144]{2,0,1:T(4,128)}), f32[3,4,6144]{2,0,1:T(4,128)S(1)}, u32[]{:S(2)}, u32[]{:S(2)}) async-start(f32[3,4,6144]{2,0,1:T(4,128)} %copy.566), calls=%async_computation | async-start | bytes 786432 | tf_op jit(solution)/shard_map/while/body/eval_jaxpr/all_to_all | solution.py:153
  23.4 10.6 %collective-permute-start = (f32[4,6144]{1,0:T(4,128)S(1)}, f32[4,6144]{1,0:T(4,128)S(1)}, u32[]{:S(2)}, u32[]{:S(2)}) collective-permute-start(f32[4,6144]{1,0:T(4,128)S(1)} %bitcast.453), channel_id=1, source_target_pairs={{4,0},{8,4},{12,8},{16,12},{20,16},{24,20},{28,24},{32,28},{36,32}... | collective-permute-start | bytes 294920 | tf_op jit(solution)/shard_map/while/body/eval_jaxpr/ppermute | solution.py:157
  31.9 3.5 %collective-permute-start.1 = (f32[4,6144]{1,0:T(4,128)S(1)}, f32[4,6144]{1,0:T(4,128)S(1)}, u32[]{:S(2)}, u32[]{:S(2)}) collective-permute-start(f32[4,6144]{1,0:T(4,128)S(1)} %bitcast.454), channel_id=1, source_target_pairs={{0,4},{4,8},{8,12},{12,16},{16,20},{20,24},{24,28},{28,32},{32,36}... | collective-permute-start | bytes 294920 | tf_op jit(solution)/shard_map/while/body/eval_jaxpr/ppermute | solution.py:156
  41.7 1.0 copy-start.4
  50.8 11.8 %all-to-all-start = ((f32[3,4,6144]{2,0,1:T(4,128)}), f32[3,4,6144]{2,0,1:T(4,128)S(1)}, u32[]{:S(2)}, u32[]{:S(2)}) async-start(f32[3,4,6144]{2,0,1:T(4,128)} %copy.566), calls=%async_computation | async-start | bytes 786432 | tf_op jit(solution)/shard_map/while/body/eval_jaxpr/all_to_all | solution.py:153
  62.8 5.9 %collective-permute-start = (f32[4,6144]{1,0:T(4,128)S(1)}, f32[4,6144]{1,0:T(4,128)S(1)}, u32[]{:S(2)}, u32[]{:S(2)}) collective-permute-start(f32[4,6144]{1,0:T(4,128)S(1)} %bitcast.453), channel_id=1, source_target_pairs={{4,0},{8,4},{12,8},{16,12},{20,16},{24,20},{28,24},{32,28},{36,32}... | collective-permute-start | bytes 294920 | tf_op jit(solution)/shard_map/while/body/eval_jaxpr/ppermute | solution.py:157
  65.4 4.6 %collective-permute-start.1 = (f32[4,6144]{1,0:T(4,128)S(1)}, f32[4,6144]{1,0:T(4,128)S(1)}, u32[]{:S(2)}, u32[]{:S(2)}) collective-permute-start(f32[4,6144]{1,0:T(4,128)S(1)} %bitcast.454), channel_id=1, source_target_pairs={{0,4},{4,8},{8,12},{12,16},{16,20},{20,24},{24,28},{28,32},{32,36}... | collective-permute-start | bytes 294920 | tf_op jit(solution)/shard_map/while/body/eval_jaxpr/ppermute | solution.py:156
  76.2 1.0 copy-start.4
  85.3 11.0 %all-to-all-start = ((f32[3,4,6144]{2,0,1:T(4,128)}), f32[3,4,6144]{2,0,1:T(4,128)S(1)}, u32[]{:S(2)}, u32[]{:S(2)}) async-start(f32[3,4,6144]{2,0,1:T(4,128)} %copy.566), calls=%async_computation | async-start | bytes 786432 | tf_op jit(solution)/shard_map/while/body/eval_jaxpr/all_to_all | solution.py:153
  96.6 6.4 %collective-permute-start = (f32[4,6144]{1,0:T(4,128)S(1)}, f32[4,6144]{1,0:T(4,128)S(1)}, u32[]{:S(2)}, u32[]{:S(2)}) collective-permute-start(f32[4,6144]{1,0:T(4,128)S(1)} %bitcast.453), channel_id=1, source_target_pairs={{4,0},{8,4},{12,8},{16,12},{20,16},{24,20},{28,24},{32,28},{36,32}... | collective-permute-start | bytes 294920 | tf_op jit(solution)/shard_map/while/body/eval_jaxpr/ppermute | solution.py:157
  98.5 5.8 %collective-permute-start.1 = (f32[4,6144]{1,0:T(4,128)S(1)}, f32[4,6144]{1,0:T(4,128)S(1)}, u32[]{:S(2)}, u32[]{:S(2)}) collective-permute-start(f32[4,6144]{1,0:T(4,128)S(1)} %bitcast.454), channel_id=1, source_target_pairs={{0,4},{4,8},{8,12},{12,16},{16,20},{20,24},{24,28},{28,32},{32,36}... | collective-permute-start | bytes 294920 | tf_op jit(solution)/shard_map/while/body/eval_jaxpr/ppermute | solution.py:156
  117.1 6.7 %copy-start.31 = (s32[1,128]{1,0:T(1,128)S(1)}, s32[1,128]{1,0:T(1,128)}, u32[]{:S(2)}) copy-start(s32[1,128]{1,0:T(1,128)} %param.20) | copy-start | bytes 1540
  118.1 8.5 %all-to-all-start.1 = ((f32[3,4,3072]{2,0,1:T(4,128)}), f32[3,4,3072]{2,0,1:T(4,128)S(1)}, u32[]{:S(2)}, u32[]{:S(2)}) async-start(f32[3,4,3072]{2,0,1:T(4,128)} %copy.405), calls=%async_computation.1 | async-start | bytes 393216 | tf_op jit(solution)/shard_map/all_to_all | solution.py:153
  121.7 3.0 %copy-start.7 = (f32[512,128]{1,0:T(8,128)S(1)}, f32[512,128]{1,0:T(8,128)}, u32[]{:S(2)}) copy-start(f32[512,128]{1,0:T(8,128)} %get-tuple-element.336) | copy-start | bytes 786436
  122.7 2.7 %copy-start.5 = (f32[3,512,128]{2,1,0:T(8,128)S(1)}, f32[3,512,128]{2,1,0:T(8,128)}, u32[]{:S(2)}) copy-start(f32[3,512,128]{2,1,0:T(8,128)} %get-tuple-element.337) | copy-start | bytes 2359300
  126.8 8.4 %collective-permute-start.2 = (f32[4,3072]{1,0:T(4,128)S(1)}, f32[4,3072]{1,0:T(4,128)S(1)}, u32[]{:S(2)}, u32[]{:S(2)}) collective-permute-start(f32[4,3072]{1,0:T(4,128)S(1)} %bitcast.465), channel_id=1, source_target_pairs={{0,4},{4,8},{8,12},{12,16},{16,20},{20,24},{24,28},{28,32},{32,36}... | collective-permute-start | bytes 147464 | tf_op jit(solution)/shard_map/ppermute | solution.py:156
  132.4 5.4 %collective-permute-start.3 = (f32[4,3072]{1,0:T(4,128)S(1)}, f32[4,3072]{1,0:T(4,128)S(1)}, u32[]{:S(2)}, u32[]{:S(2)}) collective-permute-start(f32[4,3072]{1,0:T(4,128)S(1)} %bitcast.466), channel_id=1, source_target_pairs={{4,0},{8,4},{12,8},{16,12},{20,16},{24,20},{28,24},{32,28},{36,32}... | collective-permute-start | bytes 147464 | tf_op jit(solution)/shard_map/ppermute | solution.py:157
  142.8 1.0 copy-start.15
  149.2 7.4 %all-to-all-start.2 = ((f32[4,1,642]{2,1,0:T(1,128)}), f32[4,1,642]{2,1,0:T(1,128)S(1)}, u32[]{:S(2)}, u32[]{:S(2)}) async-start(f32[4,1,642]{2,1,0:T(1,128)} %broadcast_in_dim.263), calls=%async_computation.2 | async-start | bytes 24576 | tf_op jit(solution)/shard_map/all_to_all | solution.py:253
  157.4 36.6 %all-to-all-start.3 = ((f32[128,1,2]{2,1,0:T(1,128)}), f32[128,1,2]{2,1,0:T(1,128)S(1)}, u32[]{:S(2)}, u32[]{:S(2)}) async-start(f32[128,1,2]{2,1,0:T(1,128)} %broadcast_in_dim.264), calls=%async_computation.3 | async-start | bytes 131072 | tf_op jit(solution)/shard_map/all_to_all | solution.py:256
  196.6 2.3 %copy-start.8 = (f32[3,512,128]{2,1,0:T(8,128)S(1)}, f32[3,512,128]{2,1,0:T(8,128)}, u32[]{:S(2)}) copy-start(f32[3,512,128]{2,1,0:T(8,128)} %get-tuple-element.339) | copy-start | bytes 2359300
  (24 other events, 19.4 us)

commit v5 on v1

--- a/solution.py
+++ b/solution.py
@@ -212,24 +212,26 @@
         return [total[:, k * elements:(k + 1) * elements] for k in range(number)]
 
     def paired_round(iteration, carry):
-        power, previous, latest, krylov_stack, image_stack = carry
+        power, latest, norm_stack, krylov_stack, image_stack = carry
         both = operator([power, latest])
+        power = inv_diag * both[0]
         latest = inv_diag * both[1]
         return (
-            inv_diag * both[0],
             power,
             latest,
+            lax.dynamic_update_index_in_dim(norm_stack, jnp.sum(power * power), iteration, 0),
             lax.dynamic_update_index_in_dim(krylov_stack, latest, iteration, 0),
             lax.dynamic_update_index_in_dim(image_stack, both[1], iteration, 0),
         )
 
+    rounds = max(POWER, CHEB)
     start = inv_diag * rhs
-    history = jnp.zeros((POWER,) + rhs.shape, rhs.dtype)
-    power, previous, latest, krylov_stack, image_stack = lax.fori_loop(
-        0, POWER, paired_round, (rhs, rhs, start, history, history)
-    )
-    krylov = [start] + [krylov_stack[j] for j in range(POWER)]
-    images = [image_stack[j] for j in range(POWER)] + [operator([latest])[0]]
+    history = jnp.zeros((rounds,) + rhs.shape, rhs.dtype)
+    power, latest, norm_stack, krylov_stack, image_stack = lax.fori_loop(
+        0, rounds, paired_round, (rhs, start, jnp.zeros((rounds,), rhs.dtype), history, history)
+    )
+    krylov = [start] + [krylov_stack[j] for j in range(CHEB - 1)]
+    images = [image_stack[j] for j in range(CHEB)]
 
     mass = (weights[:, None, None] * weights[None, :, None] * weights[None, None, :]).reshape(
         count * count * count, 1
@@ -237,7 +239,7 @@
     cells = coarse_inverse.shape[1]
     element_mass = jnp.stack([jnp.sum(mass * v, axis=0) for v in [rhs] + images], axis=1) / 8.0
     partial = jax.ops.segment_sum(element_mass, parent[0], num_segments=cells)
-    norms = jnp.stack([jnp.sum(power * power), jnp.sum(previous * previous)])
+    norms = jnp.stack([norm_stack[POWER - 1], norm_stack[POWER - 2]])
     narrow = lax.axis_size("narrow")
     local_block = jnp.concatenate([norms, partial.reshape(-1)])
     shared = jnp.broadcast_to(local_block[None], (narrow,) + local_block.shape)

time: 198 us -> 217 us (1.096)
  waiting for transfers between devices: 39 us -> 52 us
  other arithmetic: 16.2 us -> 20.6 us
  local copies, waits for them, and re-layouts: 47.3 us -> 50 us
  starting transfers between devices: 69.8 us -> 67.3 us
    ppermute x4, waiting for transfers between devices: 3.71 us -> 14.1 us  [neighbour_traces(): after = lax.ppermute(swapped[0], 'wide', down)]
    all_to_all x4, waiting for transfers between devices: 12.8 us -> 19.3 us  [neighbour_traces(): lax.all_to_all(outgoing, 'narrow', split_axis=1, concat_axis=1, tiled=True)]
    ppermute x4, starting transfers between devices: 14.9 us -> 9.35 us  [neighbour_traces(): after = lax.ppermute(swapped[0], 'wide', down)]
    unnamed x79 -> x38, local copies, waits for them, and re-layouts: 6.52 us -> 1.82 us
    reduce_sum x2 -> x4, other arithmetic: 1.39 us -> 5.77 us  [paired_round(): jnp.sum(power * power)]
    ppermute x4, waiting for transfers between devices: 4.17 us -> 0.01 us  [neighbour_traces(): before = lax.ppermute(swapped[2], 'wide', up)]
    concatenate x3 -> x4, local copies, waits for them, and re-layouts: 0.06 us -> 3.88 us  [operator(): field = jnp.concatenate(fields, axis=1) if number > 1 else fields[0]]
    dynamic_update_slice x0 -> x4, local copies, waits for them, and re-layouts: none -> 3.02 us  [paired_round(): lax.dynamic_update_index_in_dim(norm_stack, jnp.sum(power * power), itera...]
  transfers between devices with their start and end apart: 14 -> 14, of which waited for: 12 -> 10; matrix products, arithmetic and copies ran while one was open for 6% -> 3% of each run, Pallas kernels for 0% -> 0%
where the time goes in v5:
time: 217 us; the launch traced here: 216 us
  starting transfers between devices  67.3 us (31%)
  waiting for transfers between devices  52 us (24%)
  local copies, waits for them, and re-layouts  50 us (23%)
  matrix products  20.9 us (10%)
  other arithmetic  20.6 us (9%)
  between operations  2.72 us (1%)
    all_to_all x1, starting transfers between devices, body(): norms = jnp.sum(lax.all_to_all(spread, 'wide', 0, 0, tiled=True), axis=0)  22.2 us
    all_to_all x4, waiting for transfers between devices, neighbour_traces(): lax.all_to_all(outgoing, 'narrow', split_axis=1, concat_axis=1, tiled=True)  19.3 us
    ppermute x4, starting transfers between devices, neighbour_traces(): before = lax.ppermute(swapped[2], 'wide', up)  17.3 us
    all_to_all x4, starting transfers between devices, neighbour_traces(): lax.all_to_all(outgoing, 'narrow', split_axis=1, concat_axis=1, tiled=True)  15.2 us
    all_to_all x1, waiting for transfers between devices, body(): norms = jnp.sum(lax.all_to_all(spread, 'wide', 0, 0, tiled=True), axis=0)  14.5 us
    ppermute x4, waiting for transfers between devices, neighbour_traces(): after = lax.ppermute(swapped[0], 'wide', down)  14.1 us
    ppermute x4, starting transfers between devices, neighbour_traces(): after = lax.ppermute(swapped[0], 'wide', down)  9.35 us
    while x88, local copies, waits for them, and re-layouts  7.17 us
  transfers between devices with their start and end apart: 14, of which 10 were waited for; matrix products, arithmetic and copies ran while one was open for 3% of the time, Pallas kernels for 0%

profile of v5, /device:TPU:1, one launch (start us, length us, event | category | flops | bytes accessed | tf_op | source)
XLA Modules:
  0.0 215.6 jit_solution(10497528938080609495)
XLA Ops:
  4.1 154.5 %while.27 = (s32[]{:T(128)}, f32[512,128]{1,0:T(8,128)}, f32[512,128]{1,0:T(8,128)}, f32[4]{0:T(128)S(1)}, f32[4,512,128]{2,1,0:T(8,128)}, /*index=5*/f32[4,512,...) while((s32[]{:T(128)}, f32[512,128]{1,0:T(8,128)}, ...), condition=%wide.region_2.3_spmd.clone.clone.clone, body=%wide.region_0.2_spmd.sunk.clone.clone.clone.sunk | while | flops 80061856 | bytes 38685256 | solution.py:230
  10.3 4.8 %all-to-all-start = ((f32[3,4,6144]{2,0,1:T(4,128)}), f32[3,4,6144]{2,0,1:T(4,128)S(1)}, u32[]{:S(2)}, u32[]{:S(2)}) async-start(f32[3,4,6144]{2,0,1:T(4,128)} %copy.379), calls=%async_computation | async-start | bytes 786432 | tf_op jit(solution)/shard_map/while/body/eval_jaxpr/all_to_all | solution.py:148
  16.9 4.5 %all-to-all-done = f32[3,4,6144]{2,0,1:T(4,128)S(1)} async-done(((f32[3,4,6144]{2,0,1:T(4,128)}), f32[3,4,6144]{2,0,1:T(4,128)S(1)}, u32[]{:S(2)}, u32[]{:S(2)}) %all-to-all-start) | async-done | bytes 294944 | tf_op jit(solution)/shard_map/while/body/eval_jaxpr/all_to_all | solution.py:148
  21.7 6.2 %collective-permute-start.1 = (f32[4,6144]{1,0:T(4,128)S(1)}, f32[4,6144]{1,0:T(4,128)S(1)}, u32[]{:S(2)}, u32[]{:S(2)}) collective-permute-start(f32[4,6144]{1,0:T(4,128)S(1)} %bitcast.374), channel_id=1, source_target_pairs={{0,4},{4,8},{8,12},{12,16},{16,20},{20,24},{24,28},{28,32},{32,36}... | collective-permute-start | bytes 294920 | tf_op jit(solution)/shard_map/while/body/eval_jaxpr/ppermute | solution.py:151
  28.0 3.6 %collective-permute-start = (f32[4,6144]{1,0:T(4,128)S(1)}, f32[4,6144]{1,0:T(4,128)S(1)}, u32[]{:S(2)}, u32[]{:S(2)}) collective-permute-start(f32[4,6144]{1,0:T(4,128)S(1)} %bitcast.373), channel_id=1, source_target_pairs={{4,0},{8,4},{12,8},{16,12},{20,16},{24,20},{28,24},{32,28},{36,32}... | collective-permute-start | bytes 294920 | tf_op jit(solution)/shard_map/while/body/eval_jaxpr/ppermute | solution.py:152
  31.6 2.3 %collective-permute-done = f32[4,6144]{1,0:T(4,128)S(1)} collective-permute-done((f32[4,6144]{1,0:T(4,128)S(1)}, f32[4,6144]{1,0:T(4,128)S(1)}, u32[]{:S(2)}, u32[]{:S(2)}) %collective-permute-start) | collective-permute-done | bytes 98336 | tf_op jit(solution)/shard_map/while/body/eval_jaxpr/ppermute | solution.py:152
  51.5 3.5 %all-to-all-start = ((f32[3,4,6144]{2,0,1:T(4,128)}), f32[3,4,6144]{2,0,1:T(4,128)S(1)}, u32[]{:S(2)}, u32[]{:S(2)}) async-start(f32[3,4,6144]{2,0,1:T(4,128)} %copy.379), calls=%async_computation | async-start | bytes 786432 | tf_op jit(solution)/shard_map/while/body/eval_jaxpr/all_to_all | solution.py:148
  56.8 5.9 %all-to-all-done = f32[3,4,6144]{2,0,1:T(4,128)S(1)} async-done(((f32[3,4,6144]{2,0,1:T(4,128)}), f32[3,4,6144]{2,0,1:T(4,128)S(1)}, u32[]{:S(2)}, u32[]{:S(2)}) %all-to-all-start) | async-done | bytes 294944 | tf_op jit(solution)/shard_map/while/body/eval_jaxpr/all_to_all | solution.py:148
  63.0 2.4 %collective-permute-start.1 = (f32[4,6144]{1,0:T(4,128)S(1)}, f32[4,6144]{1,0:T(4,128)S(1)}, u32[]{:S(2)}, u32[]{:S(2)}) collective-permute-start(f32[4,6144]{1,0:T(4,128)S(1)} %bitcast.374), channel_id=1, source_target_pairs={{0,4},{4,8},{8,12},{12,16},{16,20},{20,24},{24,28},{28,32},{32,36}... | collective-permute-start | bytes 294920 | tf_op jit(solution)/shard_map/while/body/eval_jaxpr/ppermute | solution.py:151
  65.4 1.9 collective-permute-start
  67.4 3.9 %collective-permute-done = f32[4,6144]{1,0:T(4,128)S(1)} collective-permute-done((f32[4,6144]{1,0:T(4,128)S(1)}, f32[4,6144]{1,0:T(4,128)S(1)}, u32[]{:S(2)}, u32[]{:S(2)}) %collective-permute-start) | collective-permute-done | bytes 98336 | tf_op jit(solution)/shard_map/while/body/eval_jaxpr/ppermute | solution.py:152
  89.0 3.5 %all-to-all-start = ((f32[3,4,6144]{2,0,1:T(4,128)}), f32[3,4,6144]{2,0,1:T(4,128)S(1)}, u32[]{:S(2)}, u32[]{:S(2)}) async-start(f32[3,4,6144]{2,0,1:T(4,128)} %copy.379), calls=%async_computation | async-start | bytes 786432 | tf_op jit(solution)/shard_map/while/body/eval_jaxpr/all_to_all | solution.py:148
  94.2 4.4 %all-to-all-done = f32[3,4,6144]{2,0,1:T(4,128)S(1)} async-done(((f32[3,4,6144]{2,0,1:T(4,128)}), f32[3,4,6144]{2,0,1:T(4,128)S(1)}, u32[]{:S(2)}, u32[]{:S(2)}) %all-to-all-start) | async-done | bytes 294944 | tf_op jit(solution)/shard_map/while/body/eval_jaxpr/all_to_all | solution.py:148
  99.0 3.9 %collective-permute-start.1 = (f32[4,6144]{1,0:T(4,128)S(1)}, f32[4,6144]{1,0:T(4,128)S(1)}, u32[]{:S(2)}, u32[]{:S(2)}) collective-permute-start(f32[4,6144]{1,0:T(4,128)S(1)} %bitcast.374), channel_id=1, source_target_pairs={{0,4},{4,8},{8,12},{12,16},{16,20},{20,24},{24,28},{28,32},{32,36}... | collective-permute-start | bytes 294920 | tf_op jit(solution)/shard_map/while/body/eval_jaxpr/ppermute | solution.py:151
  104.9 3.9 %collective-permute-done = f32[4,6144]{1,0:T(4,128)S(1)} collective-permute-done((f32[4,6144]{1,0:T(4,128)S(1)}, f32[4,6144]{1,0:T(4,128)S(1)}, u32[]{:S(2)}, u32[]{:S(2)}) %collective-permute-start) | collective-permute-done | bytes 98336 | tf_op jit(solution)/shard_map/while/body/eval_jaxpr/ppermute | solution.py:152
  126.5 3.5 %all-to-all-start = ((f32[3,4,6144]{2,0,1:T(4,128)}), f32[3,4,6144]{2,0,1:T(4,128)S(1)}, u32[]{:S(2)}, u32[]{:S(2)}) async-start(f32[3,4,6144]{2,0,1:T(4,128)} %copy.379), calls=%async_computation | async-start | bytes 786432 | tf_op jit(solution)/shard_map/while/body/eval_jaxpr/all_to_all | solution.py:148
  131.7 4.4 %all-to-all-done = f32[3,4,6144]{2,0,1:T(4,128)S(1)} async-done(((f32[3,4,6144]{2,0,1:T(4,128)}), f32[3,4,6144]{2,0,1:T(4,128)S(1)}, u32[]{:S(2)}, u32[]{:S(2)}) %all-to-all-start) | async-done | bytes 294944 | tf_op jit(solution)/shard_map/while/body/eval_jaxpr/all_to_all | solution.py:148
  136.5 4.8 %collective-permute-start.1 = (f32[4,6144]{1,0:T(4,128)S(1)}, f32[4,6144]{1,0:T(4,128)S(1)}, u32[]{:S(2)}, u32[]{:S(2)}) collective-permute-start(f32[4,6144]{1,0:T(4,128)S(1)} %bitcast.374), channel_id=1, source_target_pairs={{0,4},{4,8},{8,12},{12,16},{16,20},{20,24},{24,28},{28,32},{32,36}... | collective-permute-start | bytes 294920 | tf_op jit(solution)/shard_map/while/body/eval_jaxpr/ppermute | solution.py:151
  141.2 1.9 collective-permute-start
  143.2 3.9 %collective-permute-done = f32[4,6144]{1,0:T(4,128)S(1)} collective-permute-done((f32[4,6144]{1,0:T(4,128)S(1)}, f32[4,6144]{1,0:T(4,128)S(1)}, u32[]{:S(2)}, u32[]{:S(2)}) %collective-permute-start) | collective-permute-done | bytes 98336 | tf_op jit(solution)/shard_map/while/body/eval_jaxpr/ppermute | solution.py:152
  164.4 3.3 %all-to-all-start.1 = ((f32[4,1,642]{2,1,0:T(1,128)}), f32[4,1,642]{2,1,0:T(1,128)S(1)}, u32[]{:S(2)}, u32[]{:S(2)}) async-start(f32[4,1,642]{2,1,0:T(1,128)} %broadcast_in_dim.251), calls=%async_computation.1 | async-start | bytes 24576 | tf_op jit(solution)/shard_map/all_to_all | solution.py:246
  167.7 4.1 %all-to-all-done.1 = f32[4,1,642]{2,1,0:T(1,128)S(1)} async-done(((f32[4,1,642]{2,1,0:T(1,128)}), f32[4,1,642]{2,1,0:T(1,128)S(1)}, u32[]{:S(2)}, u32[]{:S(2)}) %all-to-all-start.1) | async-done | bytes 10304 | tf_op jit(solution)/shard_map/all_to_all | solution.py:246
  172.8 22.2 %all-to-all-start.2 = ((f32[128,1,2]{2,1,0:T(1,128)}), f32[128,1,2]{2,1,0:T(1,128)S(1)}, u32[]{:S(2)}, u32[]{:S(2)}) async-start(f32[128,1,2]{2,1,0:T(1,128)} %broadcast_in_dim.252), calls=%async_computation.2 | async-start | bytes 131072 | tf_op jit(solution)/shard_map/all_to_all | solution.py:249
  195.5 14.5 %all-to-all-done.2 = f32[128,1,2]{2,1,0:T(1,128)S(1)} async-done(((f32[128,1,2]{2,1,0:T(1,128)}), f32[128,1,2]{2,1,0:T(1,128)S(1)}, u32[]{:S(2)}, u32[]{:S(2)}) %all-to-all-start.2) | async-done | bytes 1056 | tf_op jit(solution)/shard_map/all_to_all | solution.py:249
  (394 shorter events, 93.5 us)
Async XLA Ops:
  0.6 212.7 %copy-start = (f32[1,128,128]{2,1,0:T(8,128)S(1)}, f32[1,128,128]{2,1,0:T(8,128)}, u32[]{:S(2)}) copy-start(f32[1,128,128]{2,1,0:T(8,128)} %param.21) | copy-start | bytes 196612
  1.4 1.0 copy-start.4
  4.1 156.6 %copy-start.17 = (s32[1,128]{1,0:T(1,128)S(1)}, s32[1,128]{1,0:T(1,128)}, u32[]{:S(2)}) copy-start(s32[1,128]{1,0:T(1,128)} %param.20) | copy-start | bytes 1540
  10.3 11.1 %all-to-all-start = ((f32[3,4,6144]{2,0,1:T(4,128)}), f32[3,4,6144]{2,0,1:T(4,128)S(1)}, u32[]{:S(2)}, u32[]{:S(2)}) async-start(f32[3,4,6144]{2,0,1:T(4,128)} %copy.379), calls=%async_computation | async-start | bytes 786432 | tf_op jit(solution)/shard_map/while/body/eval_jaxpr/all_to_all | solution.py:148
  16.8 4.8 %copy-start.2 = (f32[6,8,8,256]{3,2,1,0:T(8,128)}, f32[6,8,8,256]{3,2,1,0:T(8,128)S(1)}, u32[]{:S(2)}) copy-start(f32[6,8,8,256]{3,2,1,0:T(8,128)S(1)} %fusion.138) | copy-start | bytes 1179652 | tf_op jit(solution)/shard_map/while
  21.7 9.9 %collective-permute-start.1 = (f32[4,6144]{1,0:T(4,128)S(1)}, f32[4,6144]{1,0:T(4,128)S(1)}, u32[]{:S(2)}, u32[]{:S(2)}) collective-permute-start(f32[4,6144]{1,0:T(4,128)S(1)} %bitcast.374), channel_id=1, source_target_pairs={{0,4},{4,8},{8,12},{12,16},{16,20},{20,24},{24,28},{28,32},{32,36}... | collective-permute-start | bytes 294920 | tf_op jit(solution)/shard_map/while/body/eval_jaxpr/ppermute | solution.py:151
  28.0 5.9 %collective-permute-start = (f32[4,6144]{1,0:T(4,128)S(1)}, f32[4,6144]{1,0:T(4,128)S(1)}, u32[]{:S(2)}, u32[]{:S(2)}) collective-permute-start(f32[4,6144]{1,0:T(4,128)S(1)} %bitcast.373), channel_id=1, source_target_pairs={{4,0},{8,4},{12,8},{16,12},{20,16},{24,20},{28,24},{32,28},{36,32}... | collective-permute-start | bytes 294920 | tf_op jit(solution)/shard_map/while/body/eval_jaxpr/ppermute | solution.py:152
  38.4 1.0 copy-start.3
  51.5 11.2 %all-to-all-start = ((f32[3,4,6144]{2,0,1:T(4,128)}), f32[3,4,6144]{2,0,1:T(4,128)S(1)}, u32[]{:S(2)}, u32[]{:S(2)}) async-start(f32[3,4,6144]{2,0,1:T(4,128)} %copy.379), calls=%async_computation | async-start | bytes 786432 | tf_op jit(solution)/shard_map/while/body/eval_jaxpr/all_to_all | solution.py:148
  56.7 6.3 %copy-start.2 = (f32[6,8,8,256]{3,2,1,0:T(8,128)}, f32[6,8,8,256]{3,2,1,0:T(8,128)S(1)}, u32[]{:S(2)}) copy-start(f32[6,8,8,256]{3,2,1,0:T(8,128)S(1)} %fusion.138) | copy-start | bytes 1179652 | tf_op jit(solution)/shard_map/while
  63.0 4.4 %collective-permute-start.1 = (f32[4,6144]{1,0:T(4,128)S(1)}, f32[4,6144]{1,0:T(4,128)S(1)}, u32[]{:S(2)}, u32[]{:S(2)}) collective-permute-start(f32[4,6144]{1,0:T(4,128)S(1)} %bitcast.374), channel_id=1, source_target_pairs={{0,4},{4,8},{8,12},{12,16},{16,20},{20,24},{24,28},{28,32},{32,36}... | collective-permute-start | bytes 294920 | tf_op jit(solution)/shard_map/while/body/eval_jaxpr/ppermute | solution.py:151
  65.4 5.9 %collective-permute-start = (f32[4,6144]{1,0:T(4,128)S(1)}, f32[4,6144]{1,0:T(4,128)S(1)}, u32[]{:S(2)}, u32[]{:S(2)}) collective-permute-start(f32[4,6144]{1,0:T(4,128)S(1)} %bitcast.373), channel_id=1, source_target_pairs={{4,0},{8,4},{12,8},{16,12},{20,16},{24,20},{28,24},{32,28},{36,32}... | collective-permute-start | bytes 294920 | tf_op jit(solution)/shard_map/while/body/eval_jaxpr/ppermute | solution.py:152
  89.0 9.7 %all-to-all-start = ((f32[3,4,6144]{2,0,1:T(4,128)}), f32[3,4,6144]{2,0,1:T(4,128)S(1)}, u32[]{:S(2)}, u32[]{:S(2)}) async-start(f32[3,4,6144]{2,0,1:T(4,128)} %copy.379), calls=%async_computation | async-start | bytes 786432 | tf_op jit(solution)/shard_map/while/body/eval_jaxpr/all_to_all | solution.py:148
  94.1 4.8 %copy-start.2 = (f32[6,8,8,256]{3,2,1,0:T(8,128)}, f32[6,8,8,256]{3,2,1,0:T(8,128)S(1)}, u32[]{:S(2)}) copy-start(f32[6,8,8,256]{3,2,1,0:T(8,128)S(1)} %fusion.138) | copy-start | bytes 1179652 | tf_op jit(solution)/shard_map/while
  99.0 5.9 %collective-permute-start.1 = (f32[4,6144]{1,0:T(4,128)S(1)}, f32[4,6144]{1,0:T(4,128)S(1)}, u32[]{:S(2)}, u32[]{:S(2)}) collective-permute-start(f32[4,6144]{1,0:T(4,128)S(1)} %bitcast.374), channel_id=1, source_target_pairs={{0,4},{4,8},{8,12},{12,16},{16,20},{20,24},{24,28},{28,32},{32,36}... | collective-permute-start | bytes 294920 | tf_op jit(solution)/shard_map/while/body/eval_jaxpr/ppermute | solution.py:151
  102.9 5.9 %collective-permute-start = (f32[4,6144]{1,0:T(4,128)S(1)}, f32[4,6144]{1,0:T(4,128)S(1)}, u32[]{:S(2)}, u32[]{:S(2)}) collective-permute-start(f32[4,6144]{1,0:T(4,128)S(1)} %bitcast.373), channel_id=1, source_target_pairs={{4,0},{8,4},{12,8},{16,12},{20,16},{24,20},{28,24},{32,28},{36,32}... | collective-permute-start | bytes 294920 | tf_op jit(solution)/shard_map/while/body/eval_jaxpr/ppermute | solution.py:152
  126.5 9.7 %all-to-all-start = ((f32[3,4,6144]{2,0,1:T(4,128)}), f32[3,4,6144]{2,0,1:T(4,128)S(1)}, u32[]{:S(2)}, u32[]{:S(2)}) async-start(f32[3,4,6144]{2,0,1:T(4,128)} %copy.379), calls=%async_computation | async-start | bytes 786432 | tf_op jit(solution)/shard_map/while/body/eval_jaxpr/all_to_all | solution.py:148
  131.6 4.8 %copy-start.2 = (f32[6,8,8,256]{3,2,1,0:T(8,128)}, f32[6,8,8,256]{3,2,1,0:T(8,128)S(1)}, u32[]{:S(2)}) copy-start(f32[6,8,8,256]{3,2,1,0:T(8,128)S(1)} %fusion.138) | copy-start | bytes 1179652 | tf_op jit(solution)/shard_map/while
  136.5 6.8 %collective-permute-start.1 = (f32[4,6144]{1,0:T(4,128)S(1)}, f32[4,6144]{1,0:T(4,128)S(1)}, u32[]{:S(2)}, u32[]{:S(2)}) collective-permute-start(f32[4,6144]{1,0:T(4,128)S(1)} %bitcast.374), channel_id=1, source_target_pairs={{0,4},{4,8},{8,12},{12,16},{16,20},{20,24},{24,28},{28,32},{32,36}... | collective-permute-start | bytes 294920 | tf_op jit(solution)/shard_map/while/body/eval_jaxpr/ppermute | solution.py:151
  141.2 5.9 %collective-permute-start = (f32[4,6144]{1,0:T(4,128)S(1)}, f32[4,6144]{1,0:T(4,128)S(1)}, u32[]{:S(2)}, u32[]{:S(2)}) collective-permute-start(f32[4,6144]{1,0:T(4,128)S(1)} %bitcast.373), channel_id=1, source_target_pairs={{4,0},{8,4},{12,8},{16,12},{20,16},{24,20},{28,24},{32,28},{36,32}... | collective-permute-start | bytes 294920 | tf_op jit(solution)/shard_map/while/body/eval_jaxpr/ppermute | solution.py:152
  160.6 51.9 %copy-start.5 = (f32[4,512,128]{2,1,0:T(8,128)S(1)}, f32[4,512,128]{2,1,0:T(8,128)}, u32[]{:S(2)}) copy-start(f32[4,512,128]{2,1,0:T(8,128)} %get-tuple-element.455) | copy-start | bytes 3145732
  164.4 7.4 %all-to-all-start.1 = ((f32[4,1,642]{2,1,0:T(1,128)}), f32[4,1,642]{2,1,0:T(1,128)S(1)}, u32[]{:S(2)}, u32[]{:S(2)}) async-start(f32[4,1,642]{2,1,0:T(1,128)} %broadcast_in_dim.251), calls=%async_computation.1 | async-start | bytes 24576 | tf_op jit(solution)/shard_map/all_to_all | solution.py:246
  172.8 37.2 %all-to-all-start.2 = ((f32[128,1,2]{2,1,0:T(1,128)}), f32[128,1,2]{2,1,0:T(1,128)S(1)}, u32[]{:S(2)}, u32[]{:S(2)}) async-start(f32[128,1,2]{2,1,0:T(1,128)} %broadcast_in_dim.252), calls=%async_computation.2 | async-start | bytes 131072 | tf_op jit(solution)/shard_map/all_to_all | solution.py:249
  212.5 2.2 %copy-start.7 = (f32[4,512,128]{2,1,0:T(8,128)S(1)}, f32[4,512,128]{2,1,0:T(8,128)}, u32[]{:S(2)}) copy-start(f32[4,512,128]{2,1,0:T(8,128)} %get-tuple-element.456) | copy-start | bytes 3145732
  (14 other events, 12.0 us)
